TPU v7x, 256 devices: a whole 4x4x8 slice. The times are simulated.
256 devices in a mesh: dp: 32 (over z, y), expert: 8 (over x, core).
Axes of the slice: x: 4, y: 4, z: 8, core: 2. Of those that a mesh axis runs over, the one named last changes fastest.
Arguments:
- tokens: bfloat16 [32768, 2048], P(('dp', 'expert')), may hold values from -6 to 6
- routes: int32 [32768, 2], P(('dp', 'expert')), may hold values from 0 to 127, all different within a row; in each aligned block of 128 rows (0 to 127, 128 to 255, ...) at most 4 rows name the same one
- gate_codes: int32 [32768, 2], P(('dp', 'expert')), may hold values from 1 to 1024
- w_gate: bfloat16 [256, 2048, 384], P(('dp', 'expert')), may hold values from -0.125 to 0.125
- w_up: bfloat16 [256, 2048, 384], P(('dp', 'expert')), may hold values from -0.125 to 0.125
- w_down: bfloat16 [256, 384, 2048], P(('dp', 'expert')), may hold values from -0.21875 to 0.21875
- cot: bfloat16 [32768, 2048], P(('dp', 'expert')), may hold values from -6 to 6
Outputs:
- mixed: bfloat16 [32768, 2048], P(('dp', 'expert'))
- d_tokens: bfloat16 [32768, 2048], P(('dp', 'expert'))
- d_gate: bfloat16 [256, 2048, 384], P(('dp', 'expert'))
- d_up: bfloat16 [256, 2048, 384], P(('dp', 'expert'))
- d_down: bfloat16 [256, 384, 2048], P(('dp', 'expert'))
Inputs may be any that keep to these rules, and one draw needn't show every extreme that they name: `routes`: each row names 2 different experts; among the 128 rows of one device no expert is named more than 4 times, a bound that some block reaches. `gate_codes`: the gate weight is the value divided by 1024.
All inputs are finite; a program needn't handle non-finite values.
Results may differ from a plain program's by a relative error of at most 0.012.
Values may be sent and summed in bfloat16 or wider, within the bound.
No kernel may reach another device: no remote copies, remote signals or barrier semaphores. Data moves between devices by JAX's collectives and lax.ppermute only.
A program may use at most 128 MiB of HBM per device.

v0:
```python
import jax
import jax.numpy as jnp
from jax import lax
from jax.sharding import Mesh
from jax.sharding import PartitionSpec as P

CHIPS = ("dp", "x")


def pack(rows, chips):
    return rows.reshape(chips, -1, rows.shape[1])


def to_chips(packed):
    sent = lax.all_to_all(packed, CHIPS, 0, 0, tiled=True)
    return sent.reshape(-1, packed.shape[2])


def local(tokens, routes, gate_codes, w_gate, w_up, w_down, cot):
    tok_rows, top = routes.shape
    width = tokens.shape[1]
    half = w_gate.shape[2]
    chips = lax.axis_size("dp") * lax.axis_size("x")
    pairs = tok_rows * top
    most = max(1, 2 * pairs // chips)
    slots = chips * most
    core = lax.axis_index("core")
    swap = [(0, 1), (1, 0)]
    f32 = jnp.float32

    wg_o, wu_o, wd_o = lax.ppermute((w_gate[0], w_up[0], w_down[0]), "core", swap)
    first = core == 0
    wg = jnp.where(first, jnp.concatenate([w_gate[0], wg_o], 1), jnp.concatenate([wg_o, w_gate[0]], 1))
    wu = jnp.where(first, jnp.concatenate([w_up[0], wu_o], 1), jnp.concatenate([wu_o, w_up[0]], 1))
    wd = jnp.where(first, jnp.concatenate([w_down[0], wd_o], 0), jnp.concatenate([wd_o, w_down[0]], 0))

    expert_ids = routes.reshape(pairs)
    onehot = (expert_ids[:, None] == jnp.arange(chips, dtype=jnp.int32)[None, :]).astype(jnp.int32)
    before = jnp.cumsum(onehot, axis=0) - onehot
    position = jnp.sum(before * onehot, axis=1)
    slot = expert_ids * most + position
    gates = gate_codes.reshape(pairs).astype(f32) / 1024.0
    qpairs = (
        (gates.reshape(tok_rows, top, 1) * cot.astype(f32)[:, None, :])
        .astype(jnp.bfloat16)
        .reshape(pairs, width)
    )
    pick = slot.reshape(tok_rows, top).T[:, :, None] == jnp.arange(slots, dtype=jnp.int32)[None, None, :]
    pick = pick.astype(jnp.bfloat16)
    sel_x = (pick[0] + pick[1]).reshape(tok_rows, chips, most)
    sel_q = pick.transpose(2, 1, 0).reshape(chips, most, pairs)

    sel_x2 = sel_x.reshape(tok_rows, slots)
    xs = jnp.dot(sel_x2.T, tokens, preferred_element_type=f32).astype(jnp.bfloat16)
    xrows = to_chips(pack(xs, chips))
    qs = jnp.dot(sel_q.reshape(slots, pairs), qpairs, preferred_element_type=f32).astype(jnp.bfloat16)
    qs, xrows = lax.optimization_barrier((pack(qs, chips), xrows))
    qrows = to_chips(qs)

    act = jnp.dot(xrows, wg, preferred_element_type=f32)
    upv = jnp.dot(xrows, wu, preferred_element_type=f32)
    sig = jax.nn.sigmoid(act)
    silu = act * sig
    hidden = (silu * upv).astype(jnp.bfloat16)
    outv = jnp.dot(hidden, wd, preferred_element_type=f32).astype(jnp.bfloat16)
    qrows, outv = lax.optimization_barrier((qrows, pack(outv, chips)))
    o_back = to_chips(outv)

    dhid = jnp.dot(qrows, wd.T, preferred_element_type=f32)
    dact = (dhid * upv * sig * (1.0 + act * (1.0 - sig))).astype(jnp.bfloat16)
    dupv = (dhid * silu).astype(jnp.bfloat16)
    pgrad = (
        jnp.dot(dact, wg.T, preferred_element_type=f32)
        + jnp.dot(dupv, wu.T, preferred_element_type=f32)
    ).astype(jnp.bfloat16)
    pgrad, o_back = lax.optimization_barrier((pack(pgrad, chips), o_back))
    p_back = to_chips(pgrad)

    grad_g = jnp.dot(xrows.T, dact, preferred_element_type=f32)
    grad_u = jnp.dot(xrows.T, dupv, preferred_element_type=f32)
    grad_d = jnp.dot(hidden.T, qrows, preferred_element_type=f32)
    g_lo, g_hi = grad_g[:, :half], grad_g[:, half:]
    u_lo, u_hi = grad_u[:, :half], grad_u[:, half:]
    d_lo, d_hi = grad_d[:half], grad_d[half:]
    mine = (jnp.where(first, g_lo, g_hi), jnp.where(first, u_lo, u_hi), jnp.where(first, d_lo, d_hi))
    other = (jnp.where(first, g_hi, g_lo), jnp.where(first, u_hi, u_lo), jnp.where(first, d_hi, d_lo))
    came = lax.ppermute(other, "core", swap)
    d_gate = (mine[0] + came[0]).astype(jnp.bfloat16)
    d_up = (mine[1] + came[1]).astype(jnp.bfloat16)
    d_down = (mine[2] + came[2]).astype(jnp.bfloat16)

    o_k = jnp.einsum("kts,sw->ktw", pick, o_back, preferred_element_type=f32)
    mixed = (gates.reshape(tok_rows, top).T[:, :, None] * o_k).sum(0).astype(jnp.bfloat16)
    d_tokens = jnp.dot(sel_x2, p_back, preferred_element_type=f32).astype(jnp.bfloat16)
    return (mixed, d_tokens, d_gate[None], d_up[None], d_down[None])


def solution(mesh):
    n_data = mesh.shape["dp"]
    n_group = mesh.shape["expert"]
    fine = Mesh(mesh.devices.reshape(n_data, n_group // 2, 2), ("dp", "x", "core"))
    rows = P(("dp", "x", "core"), None)
    stack = P(("dp", "x", "core"), None, None)
    return jax.shard_map(
        local,
        mesh=fine,
        in_specs=(rows, rows, rows, stack, stack, stack, rows),
        out_specs=(rows, rows, stack, stack, stack),
        check_vma=False,
    )
```

profile of v0, /device:TPU:32, one launch (start us, length us, event | category | flops | bytes accessed | tf_op | source)
XLA Modules:
  0.0 265.5 jit_solution(1220055656341720837)
XLA Ops:
  6.4 15.6 %all-to-all-start = ((bf16[128,4,2048]{2,1,0:T(4,128)(2,1)}), bf16[128,4,2048]{2,1,0:T(4,128)(2,1)}, u32[]{:S(2)}, u32[]{:S(2)}) async-start(bf16[128,4,2048]{2,1,0:T(4,128)(2,1)} %reshape.69), calls=%async_computation | async-start | bytes 4194304 | tf_op jit(solution)/shard_map/all_to_all | solution.py:15
  25.2 49.9 %all-to-all-done = bf16[128,4,2048]{2,1,0:T(4,128)(2,1)} async-done(((bf16[128,4,2048]{2,1,0:T(4,128)(2,1)}), bf16[128,4,2048]{2,1,0:T(4,128)(2,1)}, u32[]{:S(2)}, u32[]{:S(2)}) %all-to-all-start) | async-done | bytes 2097184 | tf_op jit(solution)/shard_map/all_to_all | solution.py:15
  75.1 2.5 reshape.70
  77.6 6.9 %all-to-all-start.1 = ((bf16[128,4,2048]{2,1,0:T(4,128)(2,1)}), bf16[128,4,2048]{2,1,0:T(4,128)(2,1)}, u32[]{:S(2)}, u32[]{:S(2)}) async-start(bf16[128,4,2048]{2,1,0:T(4,128)(2,1)} %reshape.68), calls=%async_computation.1 | async-start | bytes 4194304 | tf_op jit(solution)/shard_map/all_to_all | solution.py:15
  85.2 3.1 %collective-permute-done = bf16[2048,384]{1,0:T(8,128)(2,1)} collective-permute-done((bf16[2048,384]{1,0:T(8,128)(2,1)}, bf16[2048,384]{1,0:T(8,128)(2,1)}, u32[]{:S(2)}, u32[]{:S(2)}) %collective-permute-start) | collective-permute-done | bytes 1572896 | tf_op jit(solution)/shard_map/ppermute | solution.py:31
  88.4 4.7 %fusion.13 = f32[512,768]{1,0:T(8,128)S(1)} fusion(bf16[512,2048]{1,0:T(8,128)(2,1)S(1)} %reshape.70, bf16[2048,384]{1,0:T(8,128)(2,1)} %collective-permute-done, bf16[2048,384]{1,0:T(8,128)(2,1)} %bitcast.68, pred[]{:T(512)S(6)} %eq.62), kind=kOutput, calls=%fused_computation.31 | convolution fusion | flops 1624768512 | bytes 6815745 | tf_op jit(solution)/shard_map/dot_general | solution.py:60
  93.1 5.6 %multiply_convert_fusion.3 = (bf16[512,768]{1,0:T(8,128)(2,1)S(1)}, f32[512,768]{1,0:T(8,128)}) fusion(f32[512,768]{1,0:T(8,128)S(1)} %fusion.13, bf16[512,2048]{1,0:T(8,128)(2,1)S(1)} %reshape.70, bf16[2048,384]{1,0:T(8,128)(2,1)} %collective-permute-done.1, bf16[2048,384]{1,0:T(8,128)(2,1)S(1)} %bitcast.65, pred[]{:T(512)S(6)} %eq.62), kind=kOutput, calls=%fused_computation.22 | convolution fusion | flops 1627127808 | bytes 9175041 | tf_op jit(solution)/shard_map/dot_general | solution.py:61
  99.6 5.2 %convolution_convert_fusion.1 = bf16[512,2048]{1,0:T(8,128)(2,1)} fusion(bf16[512,768]{1,0:T(8,128)(2,1)S(1)} %get-tuple-element.21, bf16[384,2048]{1,0:T(8,128)(2,1)} %collective-permute-done.2, bf16[384,2048]{1,0:T(8,128)(2,1)S(1)} %bitcast.63, pred[]{:T(512)S(6)} %eq.62), kind=kOutput, calls=%fused_computation.9 | convolution fusion | flops 1625817088 | bytes 6029313 | tf_op jit(solution)/shard_map/dot_general | solution.py:65
  104.8 4.1 %reshape.72 = bf16[128,4,2048]{2,1,0:T(4,128)(2,1)} reshape(bf16[512,2048]{1,0:T(8,128)(2,1)} %convolution_convert_fusion.1) | data formatting | bytes 4194304 | tf_op jit(solution)/shard_map/reshape | solution.py:11
  108.9 27.9 %all-to-all-done.1 = bf16[128,4,2048]{2,1,0:T(4,128)(2,1)} async-done(((bf16[128,4,2048]{2,1,0:T(4,128)(2,1)}), bf16[128,4,2048]{2,1,0:T(4,128)(2,1)}, u32[]{:S(2)}, u32[]{:S(2)}) %all-to-all-start.1) | async-done | bytes 2097184 | tf_op jit(solution)/shard_map/all_to_all | solution.py:15
  136.8 4.0 %reshape.71 = bf16[512,2048]{1,0:T(8,128)(2,1)} reshape(bf16[128,4,2048]{2,1,0:T(4,128)(2,1)} %all-to-all-done.1) | data formatting | bytes 4194304 | tf_op jit(solution)/shard_map/reshape | solution.py:16
  140.8 6.9 %all-to-all-start.2 = ((bf16[128,4,2048]{2,1,0:T(4,128)(2,1)}), bf16[128,4,2048]{2,1,0:T(4,128)(2,1)}, u32[]{:S(2)}, u32[]{:S(2)}) async-start(bf16[128,4,2048]{2,1,0:T(4,128)(2,1)} %reshape.72), calls=%async_computation.2 | async-start | bytes 4194304 | tf_op jit(solution)/shard_map/all_to_all | solution.py:15
  147.7 6.8 %multiply_convert_fusion.2 = (bf16[512,768]{1,0:T(8,128)(2,1)S(1)}, bf16[512,768]{1,0:T(8,128)(2,1)S(1)}) fusion(f32[512,768]{1,0:T(8,128)} %copy-done.14, f32[512,768]{1,0:T(8,128)} %get-tuple-element.22, bf16[512,2048]{1,0:T(8,128)(2,1)} %reshape.71, bf16[384,2048]{1,0:T(8,128)(2,1)} %collective-permute-done.2, bf16[384,2048]{1,0:T(8,128)(2,1)} %bitcast.62, ...), kind=kOutput, calls=%fused_computation.21 | convolution fusion | flops 1629880320 | bytes 9961473 | tf_op jit(solution)/shard_map/dot_general | solution.py:69
  166.0 4.2 %fusion.11 = f32[512,2048]{1,0:T(8,128)S(1)} fusion(bf16[512,768]{1,0:T(8,128)(2,1)S(1)} %get-tuple-element.18, bf16[2048,384]{1,0:T(8,128)(2,1)} %collective-permute-done.1, bf16[2048,384]{1,0:T(8,128)(2,1)S(1)} %bitcast.66, pred[]{:T(512)S(6)} %eq.62), kind=kOutput, calls=%fused_computation.29 | convolution fusion | flops 1624768512 | bytes 8126465 | tf_op jit(solution)/shard_map/dot_general | solution.py:74
  170.2 4.0 %add_convert_fusion = bf16[512,2048]{1,0:T(8,128)(2,1)S(1)} fusion(f32[512,2048]{1,0:T(8,128)S(1)} %fusion.11, bf16[512,768]{1,0:T(8,128)(2,1)S(1)} %get-tuple-element.17, bf16[2048,384]{1,0:T(8,128)(2,1)} %collective-permute-done, bf16[2048,384]{1,0:T(8,128)(2,1)S(1)} %bitcast.69, pred[]{:T(512)S(6)} %eq.62), kind=kOutput, calls=%fused_computation.1 | convolution fusion | flops 1626865664 | bytes 10223617 | tf_op jit(solution)/shard_map/dot_general | solution.py:73
  174.2 4.4 %fusion.34 = f32[768,2048]{1,0:T(8,128)} fusion(bf16[512,768]{1,0:T(8,128)(2,1)S(1)} %copy-done.7, bf16[512,2048]{1,0:T(8,128)(2,1)S(1)} %copy-done.4), kind=kOutput, calls=%fused_computation.60 | convolution fusion | flops 1610612736 | bytes 9175040 | tf_op jit(solution)/shard_map/dot_general | solution.py:81
  180.9 18.5 %all-to-all-done.2 = bf16[128,4,2048]{2,1,0:T(4,128)(2,1)} async-done(((bf16[128,4,2048]{2,1,0:T(4,128)(2,1)}), bf16[128,4,2048]{2,1,0:T(4,128)(2,1)}, u32[]{:S(2)}, u32[]{:S(2)}) %all-to-all-start.2) | async-done | bytes 2097184 | tf_op jit(solution)/shard_map/all_to_all | solution.py:15
  199.4 4.0 %reshape.74 = bf16[512,2048]{1,0:T(8,128)(2,1)} reshape(bf16[128,4,2048]{2,1,0:T(4,128)(2,1)} %all-to-all-done.2) | data formatting | bytes 4194304 | tf_op jit(solution)/shard_map/reshape | solution.py:16
  203.3 7.1 %all-to-all-start.3 = ((bf16[128,4,2048]{2,1,0:T(4,128)(2,1)}), bf16[128,4,2048]{2,1,0:T(4,128)(2,1)}, u32[]{:S(2)}, u32[]{:S(2)}) async-start(bf16[128,4,2048]{2,1,0:T(4,128)(2,1)} %reshape.73), calls=%async_computation.3 | async-start | bytes 4194304 | tf_op jit(solution)/shard_map/all_to_all | solution.py:15
  210.4 3.5 %slice_select_fusion = f32[384,2048]{1,0:T(8,128)S(1)} fusion(f32[768,2048]{1,0:T(8,128)} %fusion.34, pred[]{:T(512)S(6)} %eq.62), kind=kLoop, calls=%fused_computation.10 | loop fusion | flops 786432 | bytes 9437185 | tf_op jit(solution)/shard_map/jit(_where)/select_n | solution.py:86
  214.5 4.3 %fusion.1 = bf16[1,2048,384]{2,1,0:T(8,128)(2,1)} fusion(f32[2048,384]{1,0:T(8,128)} %collective-permute-done.3, f32[2048,768]{1,0:T(8,128)S(1)} %bitcast.51, pred[]{:T(512)S(6)} %eq.62), kind=kLoop, calls=%fused_computation.17 | loop fusion | flops 2359296 | bytes 11010049 | tf_op jit(solution)/shard_map/broadcast_in_dim | solution.py:95
  218.7 3.9 %fusion.2 = bf16[1,2048,384]{2,1,0:T(8,128)(2,1)} fusion(f32[2048,384]{1,0:T(8,128)} %collective-permute-done.4, f32[2048,768]{1,0:T(8,128)S(1)} %bitcast.53, pred[]{:T(512)S(6)} %eq.62), kind=kLoop, calls=%fused_computation.18 | loop fusion | flops 2359296 | bytes 11010049 | tf_op jit(solution)/shard_map/broadcast_in_dim | solution.py:95
  226.2 35.5 %all-to-all-done.3 = bf16[128,4,2048]{2,1,0:T(4,128)(2,1)} async-done(((bf16[128,4,2048]{2,1,0:T(4,128)(2,1)}), bf16[128,4,2048]{2,1,0:T(4,128)(2,1)}, u32[]{:S(2)}, u32[]{:S(2)}) %all-to-all-start.3) | async-done | bytes 2097184 | tf_op jit(solution)/shard_map/all_to_all | solution.py:15
  261.7 2.5 reshape.75
  (86 shorter events, 29.4 us)
Async XLA Ops:
  6.4 15.6 %copy-start.8 = (bf16[128,2048]{1,0:T(8,128)(2,1)S(1)}, bf16[128,2048]{1,0:T(8,128)(2,1)}, u32[]{:S(2)}) copy-start(bf16[128,2048]{1,0:T(8,128)(2,1)} %param.13) | copy-start | bytes 1572868
  6.4 15.7 %copy-start.9 = (s32[128,2]{0,1:T(2,128)S(1)}, s32[128,2]{0,1:T(2,128)}, u32[]{:S(2)}) copy-start(s32[128,2]{0,1:T(2,128)} %param.9) | copy-start | bytes 3076
  6.4 68.7 %all-to-all-start = ((bf16[128,4,2048]{2,1,0:T(4,128)(2,1)}), bf16[128,4,2048]{2,1,0:T(4,128)(2,1)}, u32[]{:S(2)}, u32[]{:S(2)}) async-start(bf16[128,4,2048]{2,1,0:T(4,128)(2,1)} %reshape.69), calls=%async_computation | async-start | bytes 4194304 | tf_op jit(solution)/shard_map/all_to_all | solution.py:15
  77.6 59.2 %all-to-all-start.1 = ((bf16[128,4,2048]{2,1,0:T(4,128)(2,1)}), bf16[128,4,2048]{2,1,0:T(4,128)(2,1)}, u32[]{:S(2)}, u32[]{:S(2)}) async-start(bf16[128,4,2048]{2,1,0:T(4,128)(2,1)} %reshape.68), calls=%async_computation.1 | async-start | bytes 4194304 | tf_op jit(solution)/shard_map/all_to_all | solution.py:15
  84.5 3.8 %collective-permute-start = (bf16[2048,384]{1,0:T(8,128)(2,1)}, bf16[2048,384]{1,0:T(8,128)(2,1)}, u32[]{:S(2)}, u32[]{:S(2)}) collective-permute-start(bf16[2048,384]{1,0:T(8,128)(2,1)} %bitcast.67), channel_id=1, source_target_pairs={{0,1},{1,0},{2,3},{3,2},{4,5},{5,4},{6,7},{7,6},{8,9},{9,8},{10,11... | collective-permute-start | bytes 4718600 | tf_op jit(solution)/shard_map/ppermute | solution.py:31
  84.6 8.5 %collective-permute-start.1 = (bf16[2048,384]{1,0:T(8,128)(2,1)}, bf16[2048,384]{1,0:T(8,128)(2,1)}, u32[]{:S(2)}, u32[]{:S(2)}) collective-permute-start(bf16[2048,384]{1,0:T(8,128)(2,1)} %bitcast.64), channel_id=1, source_target_pairs={{0,1},{1,0},{2,3},{3,2},{4,5},{5,4},{6,7},{7,6},{8,9},{9,8},{10,11... | collective-permute-start | bytes 4718600 | tf_op jit(solution)/shard_map/ppermute | solution.py:31
  85.1 13.6 %collective-permute-start.2 = (bf16[384,2048]{1,0:T(8,128)(2,1)}, bf16[384,2048]{1,0:T(8,128)(2,1)}, u32[]{:S(2)}, u32[]{:S(2)}) collective-permute-start(bf16[384,2048]{1,0:T(8,128)(2,1)} %bitcast.61), channel_id=1, source_target_pairs={{0,1},{1,0},{2,3},{3,2},{4,5},{5,4},{6,7},{7,6},{8,9},{9,8},{10,11... | collective-permute-start | bytes 4718600 | tf_op jit(solution)/shard_map/ppermute | solution.py:31
  85.2 7.9 %copy-start.11 = (bf16[1,2048,384]{2,1,0:T(8,128)(2,1)S(1)}, bf16[1,2048,384]{2,1,0:T(8,128)(2,1)}, u32[]{:S(2)}) copy-start(bf16[1,2048,384]{2,1,0:T(8,128)(2,1)} %param.11) | copy-start | bytes 4718596
  93.1 5.6 %copy-start.14 = (f32[512,768]{1,0:T(8,128)}, f32[512,768]{1,0:T(8,128)S(1)}, u32[]{:S(2)}) copy-start(f32[512,768]{1,0:T(8,128)S(1)} %fusion.13) | copy-start | bytes 4718596
  93.1 6.5 %copy-start.10 = (bf16[1,384,2048]{2,1,0:T(8,128)(2,1)S(1)}, bf16[1,384,2048]{2,1,0:T(8,128)(2,1)}, u32[]{:S(2)}) copy-start(bf16[1,384,2048]{2,1,0:T(8,128)(2,1)} %param.12) | copy-start | bytes 4718596
  140.8 58.5 %all-to-all-start.2 = ((bf16[128,4,2048]{2,1,0:T(4,128)(2,1)}), bf16[128,4,2048]{2,1,0:T(4,128)(2,1)}, u32[]{:S(2)}, u32[]{:S(2)}) async-start(bf16[128,4,2048]{2,1,0:T(4,128)(2,1)} %reshape.72), calls=%async_computation.2 | async-start | bytes 4194304 | tf_op jit(solution)/shard_map/all_to_all | solution.py:15
  160.0 54.3 %collective-permute-start.3 = (f32[2048,384]{1,0:T(8,128)}, f32[2048,384]{1,0:T(8,128)}, u32[]{:S(2)}, u32[]{:S(2)}) collective-permute-start(f32[2048,384]{1,0:T(8,128)} %slice_select_fusion.2), channel_id=1, source_target_pairs={{0,1},{1,0},{2,3},{3,2},{4,5},{5,4},{6,7},{7,6},{8,9},{9,8},{10,11... | collective-permute-start | bytes 9437192 | tf_op jit(solution)/shard_map/ppermute | solution.py:87
  161.9 4.1 %copy-start.12 = (bf16[1,2048,384]{2,1,0:T(8,128)(2,1)S(1)}, bf16[1,2048,384]{2,1,0:T(8,128)(2,1)}, u32[]{:S(2)}) copy-start(bf16[1,2048,384]{2,1,0:T(8,128)(2,1)} %param.11) | copy-start | bytes 4718596
  165.5 4.7 %copy-start.13 = (bf16[1,2048,384]{2,1,0:T(8,128)(2,1)S(1)}, bf16[1,2048,384]{2,1,0:T(8,128)(2,1)}, u32[]{:S(2)}) copy-start(bf16[1,2048,384]{2,1,0:T(8,128)(2,1)} %param.10) | copy-start | bytes 4718596
  165.5 53.2 %collective-permute-start.4 = (f32[2048,384]{1,0:T(8,128)}, f32[2048,384]{1,0:T(8,128)}, u32[]{:S(2)}, u32[]{:S(2)}) collective-permute-start(f32[2048,384]{1,0:T(8,128)} %slice_select_fusion.1), channel_id=1, source_target_pairs={{0,1},{1,0},{2,3},{3,2},{4,5},{5,4},{6,7},{7,6},{8,9},{9,8},{10,11... | collective-permute-start | bytes 9437192 | tf_op jit(solution)/shard_map/ppermute | solution.py:87
  170.2 4.0 %copy-start.4 = (bf16[512,2048]{1,0:T(8,128)(2,1)S(1)}, bf16[512,2048]{1,0:T(8,128)(2,1)}, u32[]{:S(2)}) copy-start(bf16[512,2048]{1,0:T(8,128)(2,1)} %reshape.71) | copy-start | bytes 6291460
  203.3 11.0 %slice-start = ((s8[6291456]{0:T(1024)(128)(4,1)}), s8[2097152]{0:T(1024)(128)(4,1)S(1)}, s32[]{:S(2)}) async-start(s8[6291456]{0:T(1024)(128)(4,1)} %bitcast.50), calls=%async_computation.4 | async-start | bytes 4194304
  203.3 58.4 %all-to-all-start.3 = ((bf16[128,4,2048]{2,1,0:T(4,128)(2,1)}), bf16[128,4,2048]{2,1,0:T(4,128)(2,1)}, u32[]{:S(2)}, u32[]{:S(2)}) async-start(bf16[128,4,2048]{2,1,0:T(4,128)(2,1)} %reshape.73), calls=%async_computation.3 | async-start | bytes 4194304 | tf_op jit(solution)/shard_map/all_to_all | solution.py:15
  210.4 4.0 %slice-start.1 = ((s8[6291456]{0:T(1024)(128)(4,1)}), s8[4194304]{0:T(1024)(128)(4,1)S(1)}, s32[]{:S(2)}) async-start(s8[6291456]{0:T(1024)(128)(4,1)} %bitcast.50), calls=%async_computation.5 | async-start | bytes 8388608
  210.4 8.3 %slice-start.2 = ((s8[6291456]{0:T(1024)(128)(4,1)}), s8[4194304]{0:T(1024)(128)(4,1)S(1)}, s32[]{:S(2)}) async-start(s8[6291456]{0:T(1024)(128)(4,1)} %bitcast.52), calls=%async_computation.6 | async-start | bytes 8388608
  213.9 4.8 %slice-start.3 = ((s8[6291456]{0:T(1024)(128)(4,1)}), s8[2097152]{0:T(1024)(128)(4,1)S(1)}, s32[]{:S(2)}) async-start(s8[6291456]{0:T(1024)(128)(4,1)} %bitcast.52), calls=%async_computation.7 | async-start | bytes 4194304
  213.9 8.7 %collective-permute-start.5 = (f32[384,2048]{1,0:T(8,128)S(1)}, f32[384,2048]{1,0:T(8,128)S(1)}, u32[]{:S(2)}, u32[]{:S(2)}) collective-permute-start(f32[384,2048]{1,0:T(8,128)S(1)} %slice_select_fusion), channel_id=1, source_target_pairs={{0,1},{1,0},{2,3},{3,2},{4,5},{5,4},{6,7},{7,6},{8,9},{9,8},{10,11... | collective-permute-start | bytes 9437192 | tf_op jit(solution)/shard_map/ppermute | solution.py:87
  214.5 8.1 %slice-start.4 = ((s8[6291456]{0:T(1024)(128)(4,1)}), s8[4194304]{0:T(1024)(128)(4,1)S(1)}, s32[]{:S(2)}) async-start(s8[6291456]{0:T(1024)(128)(4,1)} %bitcast.54), calls=%async_computation.8 | async-start | bytes 8388608
  224.5 41.0 %copy-start.1 = (bf16[128,2048]{1,0:T(8,128)(2,1)S(1)}, bf16[128,2048]{1,0:T(8,128)(2,1)}, u32[]{:S(2)}) copy-start(bf16[128,2048]{1,0:T(8,128)(2,1)} %param.7) | copy-start | bytes 1572868
  (7 other events, 20.8 us)
where the time goes:
time: 266 us
  waiting for transfers between devices  135 us (51%)
  matrix products  43 us (16%)
  starting transfers between devices  37.9 us (14%)
  local copies, waits for them, and re-layouts  29.5 us (11%)
  other arithmetic  19 us (7%)
    all_to_all x4, waiting for transfers between devices, to_chips(): sent = lax.all_to_all(packed, CHIPS, 0, 0, tiled=True)  132 us
    all_to_all x4, starting transfers between devices, to_chips(): sent = lax.all_to_all(packed, CHIPS, 0, 0, tiled=True)  36.4 us
    reshape x4, local copies, waits for them, and re-layouts, to_chips(): return sent.reshape(-1, packed.shape[2])  13.1 us
    reshape x4, local copies, waits for them, and re-layouts, pack(): return rows.reshape(chips, -1, rows.shape[1])  10.8 us
    broadcast_in_dim x3, other arithmetic, local(): return (mixed, d_tokens, d_gate[None], d_up[None], d_down[None])  10 us
    dot_general x1, matrix products, local(): dhid = jnp.dot(qrows, wd.T, preferred_element_type=f32)  6.83 us
    dot_general x1, matrix products, local(): upv = jnp.dot(xrows, wu, preferred_element_type=f32)  5.57 us
  transfers between devices with their start and end apart: 10, of which 5 were waited for; matrix products, arithmetic and copies ran while one was open for 27% of the time, Pallas kernels for 0%

commit v1 on v0

--- a/solution.py
+++ b/solution.py
@@ -12,8 +12,11 @@
 
 
 def to_chips(packed):
-    sent = lax.all_to_all(packed, CHIPS, 0, 0, tiled=True)
-    return sent.reshape(-1, packed.shape[2])
+    return lax.all_to_all(packed, CHIPS, 0, 0, tiled=True)
+
+
+def unpack(sent):
+    return sent.reshape(-1, sent.shape[2])
 
 
 def local(tokens, routes, gate_codes, w_gate, w_up, w_down, cot):
@@ -55,6 +58,7 @@
     xrows = to_chips(pack(xs, chips))
     qs = jnp.dot(sel_q.reshape(slots, pairs), qpairs, preferred_element_type=f32).astype(jnp.bfloat16)
     qs, xrows = lax.optimization_barrier((pack(qs, chips), xrows))
+    xrows = unpack(xrows)
     qrows = to_chips(qs)
 
     act = jnp.dot(xrows, wg, preferred_element_type=f32)
@@ -64,6 +68,7 @@
     hidden = (silu * upv).astype(jnp.bfloat16)
     outv = jnp.dot(hidden, wd, preferred_element_type=f32).astype(jnp.bfloat16)
     qrows, outv = lax.optimization_barrier((qrows, pack(outv, chips)))
+    qrows = unpack(qrows)
     o_back = to_chips(outv)
 
     dhid = jnp.dot(qrows, wd.T, preferred_element_type=f32)
@@ -74,7 +79,8 @@
         + jnp.dot(dupv, wu.T, preferred_element_type=f32)
     ).astype(jnp.bfloat16)
     pgrad, o_back = lax.optimization_barrier((pack(pgrad, chips), o_back))
-    p_back = to_chips(pgrad)
+    o_back = unpack(o_back)
+    p_back = unpack(to_chips(pgrad))
 
     grad_g = jnp.dot(xrows.T, dact, preferred_element_type=f32)
     grad_u = jnp.dot(xrows.T, dupv, preferred_element_type=f32)

time: 266 us -> 261 us (0.981)
  waiting for transfers between devices: 135 us -> 119 us
  local copies, waits for them, and re-layouts: 29.5 us -> 35.1 us
  matrix products: 43 us -> 48.3 us
    all_to_all x4, waiting for transfers between devices: 132 us -> 118 us  [to_chips(): return lax.all_to_all(packed, CHIPS, 0, 0, tiled=True)]
    reshape x4, local copies, waits for them, and re-layouts: 10.8 us -> 14.6 us  [pack(): return rows.reshape(chips, -1, rows.shape[1])]
  transfers between devices with their start and end apart: 10 -> 10, of which waited for: 5 -> 5; matrix products, arithmetic and copies ran while one was open for 27% -> 32% of each run, Pallas kernels for 0% -> 0%
where the time goes in v1:
time: 261 us; the launch traced here: 260 us
  waiting for transfers between devices  119 us (46%)
  matrix products  48.3 us (19%)
  starting transfers between devices  36.4 us (14%)
  local copies, waits for them, and re-layouts  35.1 us (13%)
  other arithmetic  20.4 us (8%)
    all_to_all x4, waiting for transfers between devices, to_chips(): return lax.all_to_all(packed, CHIPS, 0, 0, tiled=True)  118 us
    all_to_all x4, starting transfers between devices, to_chips(): return lax.all_to_all(packed, CHIPS, 0, 0, tiled=True)  35.3 us
    reshape x4, local copies, waits for them, and re-layouts, pack(): return rows.reshape(chips, -1, rows.shape[1])  14.6 us
    reshape x4, local copies, waits for them, and re-layouts, unpack(): return sent.reshape(-1, sent.shape[2])  12.6 us
    broadcast_in_dim x3, other arithmetic, local(): return (mixed, d_tokens, d_gate[None], d_up[None], d_down[None])  11.3 us
    unnamed x44, local copies, waits for them, and re-layouts  7.24 us
    dot_general x1, matrix products, local(): upv = jnp.dot(xrows, wu, preferred_element_type=f32)  5.57 us
    dot_general x1, matrix products, local(): jnp.dot(dact, wg.T, preferred_element_type=f32)  5.27 us
  transfers between devices with their start and end apart: 10, of which 5 were waited for; matrix products, arithmetic and copies ran while one was open for 32% of the time, Pallas kernels for 0%

profile of v1, /device:TPU:32, one launch (start us, length us, event | category | flops | bytes accessed | tf_op | source)
XLA Modules:
  0.0 259.8 jit_solution(17624885115443848107)
XLA Ops:
  6.4 15.1 %all-to-all-start = ((bf16[128,4,2048]{2,1,0:T(4,128)(2,1)}), bf16[128,4,2048]{2,1,0:T(4,128)(2,1)S(1)}, u32[]{:S(2)}, u32[]{:S(2)}) async-start(bf16[128,4,2048]{2,1,0:T(4,128)(2,1)} %reshape.69), calls=%async_computation | async-start | bytes 4194304 | tf_op jit(solution)/shard_map/all_to_all | solution.py:15
  23.8 4.1 %reshape.68 = bf16[128,4,2048]{2,1,0:T(4,128)(2,1)} reshape(bf16[512,2048]{1,0:T(8,128)(2,1)} %bitcast_convert_fusion) | data formatting | bytes 4194304 | tf_op jit(solution)/shard_map/reshape | solution.py:11
  28.0 47.0 %all-to-all-done = bf16[128,4,2048]{2,1,0:T(4,128)(2,1)S(1)} async-done(((bf16[128,4,2048]{2,1,0:T(4,128)(2,1)}), bf16[128,4,2048]{2,1,0:T(4,128)(2,1)S(1)}, u32[]{:S(2)}, u32[]{:S(2)}) %all-to-all-start) | async-done | bytes 2097184 | tf_op jit(solution)/shard_map/all_to_all | solution.py:15
  75.0 6.9 %all-to-all-start.1 = ((bf16[128,4,2048]{2,1,0:T(4,128)(2,1)}), bf16[128,4,2048]{2,1,0:T(4,128)(2,1)}, u32[]{:S(2)}, u32[]{:S(2)}) async-start(bf16[128,4,2048]{2,1,0:T(4,128)(2,1)} %reshape.68), calls=%async_computation.1 | async-start | bytes 4194304 | tf_op jit(solution)/shard_map/all_to_all | solution.py:15
  85.7 4.8 %fusion.10 = f32[512,768]{1,0:T(8,128)S(1)} fusion(bf16[512,2048]{1,0:T(8,128)(2,1)S(1)} %reshape.70, bf16[2048,384]{1,0:T(8,128)(2,1)} %collective-permute-done, bf16[2048,384]{1,0:T(8,128)(2,1)} %bitcast.62, pred[]{:T(512)S(6)} %eq.62), kind=kOutput, calls=%fused_computation.30 | convolution fusion | flops 1624768512 | bytes 6815745 | tf_op jit(solution)/shard_map/dot_general | solution.py:64
  90.6 5.6 %multiply_convert_fusion.3 = (bf16[512,768]{1,0:T(8,128)(2,1)S(1)}, f32[512,768]{1,0:T(8,128)}) fusion(f32[512,768]{1,0:T(8,128)S(1)} %fusion.10, bf16[512,2048]{1,0:T(8,128)(2,1)S(1)} %reshape.70, bf16[2048,384]{1,0:T(8,128)(2,1)} %collective-permute-done.1, bf16[2048,384]{1,0:T(8,128)(2,1)S(1)} %bitcast.59, pred[]{:T(512)S(6)} %eq.62), kind=kOutput, calls=%fused_computation.21 | convolution fusion | flops 1627127808 | bytes 9175041 | tf_op jit(solution)/shard_map/dot_general | solution.py:65
  97.1 5.2 %convolution_convert_fusion.1 = bf16[512,2048]{1,0:T(8,128)(2,1)} fusion(bf16[512,768]{1,0:T(8,128)(2,1)S(1)} %get-tuple-element.21, bf16[384,2048]{1,0:T(8,128)(2,1)} %collective-permute-done.2, bf16[384,2048]{1,0:T(8,128)(2,1)S(1)} %bitcast.56, pred[]{:T(512)S(6)} %eq.62), kind=kOutput, calls=%fused_computation.9 | convolution fusion | flops 1625817088 | bytes 6029313 | tf_op jit(solution)/shard_map/dot_general | solution.py:69
  102.2 4.1 %reshape.71 = bf16[128,4,2048]{2,1,0:T(4,128)(2,1)} reshape(bf16[512,2048]{1,0:T(8,128)(2,1)} %convolution_convert_fusion.1) | data formatting | bytes 4194304 | tf_op jit(solution)/shard_map/reshape | solution.py:11
  106.4 27.8 %all-to-all-done.1 = bf16[128,4,2048]{2,1,0:T(4,128)(2,1)} async-done(((bf16[128,4,2048]{2,1,0:T(4,128)(2,1)}), bf16[128,4,2048]{2,1,0:T(4,128)(2,1)}, u32[]{:S(2)}, u32[]{:S(2)}) %all-to-all-start.1) | async-done | bytes 2097184 | tf_op jit(solution)/shard_map/all_to_all | solution.py:15
  134.1 4.1 %reshape.72 = bf16[512,2048]{1,0:T(8,128)(2,1)} reshape(bf16[128,4,2048]{2,1,0:T(4,128)(2,1)} %all-to-all-done.1) | data formatting | bytes 4194304 | tf_op jit(solution)/shard_map/reshape | solution.py:19
  138.2 6.9 %all-to-all-start.2 = ((bf16[128,4,2048]{2,1,0:T(4,128)(2,1)}), bf16[128,4,2048]{2,1,0:T(4,128)(2,1)}, u32[]{:S(2)}, u32[]{:S(2)}) async-start(bf16[128,4,2048]{2,1,0:T(4,128)(2,1)} %reshape.71), calls=%async_computation.2 | async-start | bytes 4194304 | tf_op jit(solution)/shard_map/all_to_all | solution.py:15
  145.1 3.7 %fusion.31 = f32[768,2048]{1,0:T(8,128)S(1)} fusion(bf16[512,768]{1,0:T(8,128)(2,1)} %copy-done.6, bf16[512,2048]{1,0:T(8,128)(2,1)} %reshape.72), kind=kOutput, calls=%fused_computation.59 | convolution fusion | flops 1610612736 | bytes 9175040 | tf_op jit(solution)/shard_map/dot_general | solution.py:87
  155.1 4.3 %multiply_convert_fusion.2 = (bf16[512,768]{1,0:T(8,128)(2,1)S(1)}, bf16[512,768]{1,0:T(8,128)(2,1)S(1)}) fusion(f32[512,768]{1,0:T(8,128)S(1)} %copy-done.15, f32[512,768]{1,0:T(8,128)S(1)} %copy-done.16, bf16[512,2048]{1,0:T(8,128)(2,1)S(1)} %copy-done.5, bf16[384,2048]{1,0:T(8,128)(2,1)} %collective-permute-done.2, bf16[384,2048]{1,0:T(8,128)(2,1)S(1)} %bitcast.57, ...), kind=kOutput, calls=%fused_computation.20 | convolution fusion | flops 1629880320 | bytes 9961473 | tf_op jit(solution)/shard_map/dot_general | solution.py:74
  164.8 4.1 %fusion.8 = f32[512,2048]{1,0:T(8,128)S(1)} fusion(bf16[512,768]{1,0:T(8,128)(2,1)S(1)} %get-tuple-element.18, bf16[2048,384]{1,0:T(8,128)(2,1)} %collective-permute-done.1, bf16[2048,384]{1,0:T(8,128)(2,1)S(1)} %bitcast.60, pred[]{:T(512)S(6)} %eq.62), kind=kOutput, calls=%fused_computation.28 | convolution fusion | flops 1624768512 | bytes 8126465 | tf_op jit(solution)/shard_map/dot_general | solution.py:79
  168.9 5.3 %add_convert_fusion = bf16[512,2048]{1,0:T(8,128)(2,1)} fusion(f32[512,2048]{1,0:T(8,128)S(1)} %fusion.8, bf16[512,768]{1,0:T(8,128)(2,1)S(1)} %get-tuple-element.17, bf16[2048,384]{1,0:T(8,128)(2,1)} %collective-permute-done, bf16[2048,384]{1,0:T(8,128)(2,1)S(1)} %bitcast.63, pred[]{:T(512)S(6)} %eq.62), kind=kOutput, calls=%fused_computation.1 | convolution fusion | flops 1626865664 | bytes 10223617 | tf_op jit(solution)/shard_map/dot_general | solution.py:78
  174.2 4.4 %fusion.30 = f32[2048,768]{1,0:T(8,128)} fusion(bf16[512,2048]{1,0:T(8,128)(2,1)S(1)} %reshape.70, bf16[512,768]{1,0:T(8,128)(2,1)S(1)} %get-tuple-element.18), kind=kOutput, calls=%fused_computation.58 | convolution fusion | flops 1610612736 | bytes 9175040 | tf_op jit(solution)/shard_map/dot_general | solution.py:86
  178.7 4.1 %reshape.73 = bf16[128,4,2048]{2,1,0:T(4,128)(2,1)} reshape(bf16[512,2048]{1,0:T(8,128)(2,1)} %add_convert_fusion) | data formatting | bytes 4194304 | tf_op jit(solution)/shard_map/reshape | solution.py:11
  182.8 14.0 %all-to-all-done.2 = bf16[128,4,2048]{2,1,0:T(4,128)(2,1)} async-done(((bf16[128,4,2048]{2,1,0:T(4,128)(2,1)}), bf16[128,4,2048]{2,1,0:T(4,128)(2,1)}, u32[]{:S(2)}, u32[]{:S(2)}) %all-to-all-start.2) | async-done | bytes 2097184 | tf_op jit(solution)/shard_map/all_to_all | solution.py:15
  196.8 6.5 %all-to-all-start.3 = ((bf16[128,4,2048]{2,1,0:T(4,128)(2,1)}), bf16[128,4,2048]{2,1,0:T(4,128)(2,1)S(1)}, u32[]{:S(2)}, u32[]{:S(2)}) async-start(bf16[128,4,2048]{2,1,0:T(4,128)(2,1)} %reshape.73), calls=%async_computation.3 | async-start | bytes 4194304 | tf_op jit(solution)/shard_map/all_to_all | solution.py:15
  207.0 5.8 %fusion.2 = bf16[1,384,2048]{2,1,0:T(8,128)(2,1)} fusion(f32[384,2048]{1,0:T(8,128)} %collective-permute-done.5, f32[768,2048]{1,0:T(8,128)} %copy-done.3, pred[]{:T(512)S(6)} %eq.62), kind=kLoop, calls=%fused_computation.18 | loop fusion | flops 2359296 | bytes 11010049 | tf_op jit(solution)/shard_map/broadcast_in_dim | solution.py:101
  212.8 3.9 %fusion = bf16[1,2048,384]{2,1,0:T(8,128)(2,1)} fusion(f32[2048,384]{1,0:T(8,128)} %collective-permute-done.3, f32[2048,768]{1,0:T(8,128)S(1)} %bitcast.47, pred[]{:T(512)S(6)} %eq.62), kind=kLoop, calls=%fused_computation.16 | loop fusion | flops 2359296 | bytes 11010049 | tf_op jit(solution)/shard_map/broadcast_in_dim | solution.py:101
  218.3 4.0 %reshape.77 = bf16[512,2048,1]{1,0,2:T(8,128)(2,1)} reshape(bf16[128,4,2048]{2,1,0:T(4,128)(2,1)} %all-to-all-done.2) | data formatting | bytes 4194304 | tf_op jit(solution)/shard_map/reshape | solution.py:19
  222.3 3.4 %fusion.4 = bf16[128,2048]{1,0:T(8,128)(2,1)} fusion(bf16[512,2048,1]{1,0,2:T(8,128)(2,1)} %reshape.77, f32[2,128]{1,0:T(2,128)S(1)} %get-tuple-element.19, s32[2,128]{1,0:T(2,128)S(1)} %bitcast.54), kind=kOutput, calls=%fused_computation.24 | convolution fusion | flops 537788416 | bytes 2623488 | tf_op jit(solution)/shard_map/kts,sw->ktw/dot_general | solution.py:98
  225.7 29.2 %all-to-all-done.3 = bf16[128,4,2048]{2,1,0:T(4,128)(2,1)S(1)} async-done(((bf16[128,4,2048]{2,1,0:T(4,128)(2,1)}), bf16[128,4,2048]{2,1,0:T(4,128)(2,1)S(1)}, u32[]{:S(2)}, u32[]{:S(2)}) %all-to-all-start.3) | async-done | bytes 2097184 | tf_op jit(solution)/shard_map/all_to_all | solution.py:15
  (85 shorter events, 34.5 us)
Async XLA Ops:
  6.4 15.2 %copy-start.7 = (bf16[128,2048]{1,0:T(8,128)(2,1)S(1)}, bf16[128,2048]{1,0:T(8,128)(2,1)}, u32[]{:S(2)}) copy-start(bf16[128,2048]{1,0:T(8,128)(2,1)} %param.13) | copy-start | bytes 1572868
  6.4 15.3 %copy-start.8 = (s32[128,2]{0,1:T(2,128)S(1)}, s32[128,2]{0,1:T(2,128)}, u32[]{:S(2)}) copy-start(s32[128,2]{0,1:T(2,128)} %param.9) | copy-start | bytes 3076
  6.4 68.6 %all-to-all-start = ((bf16[128,4,2048]{2,1,0:T(4,128)(2,1)}), bf16[128,4,2048]{2,1,0:T(4,128)(2,1)S(1)}, u32[]{:S(2)}, u32[]{:S(2)}) async-start(bf16[128,4,2048]{2,1,0:T(4,128)(2,1)} %reshape.69), calls=%async_computation | async-start | bytes 4194304 | tf_op jit(solution)/shard_map/all_to_all | solution.py:15
  75.0 7.6 %copy-start.4 = (bf16[128,4,2048]{2,1,0:T(4,128)(2,1)}, bf16[128,4,2048]{2,1,0:T(4,128)(2,1)S(1)}, u32[]{:S(2)}) copy-start(bf16[128,4,2048]{2,1,0:T(4,128)(2,1)S(1)} %all-to-all-done) | copy-start | bytes 6291460
  75.0 59.1 %all-to-all-start.1 = ((bf16[128,4,2048]{2,1,0:T(4,128)(2,1)}), bf16[128,4,2048]{2,1,0:T(4,128)(2,1)}, u32[]{:S(2)}, u32[]{:S(2)}) async-start(bf16[128,4,2048]{2,1,0:T(4,128)(2,1)} %reshape.68), calls=%async_computation.1 | async-start | bytes 4194304 | tf_op jit(solution)/shard_map/all_to_all | solution.py:15
  81.9 3.8 %collective-permute-start = (bf16[2048,384]{1,0:T(8,128)(2,1)}, bf16[2048,384]{1,0:T(8,128)(2,1)}, u32[]{:S(2)}, u32[]{:S(2)}) collective-permute-start(bf16[2048,384]{1,0:T(8,128)(2,1)} %bitcast.61), channel_id=1, source_target_pairs={{0,1},{1,0},{2,3},{3,2},{4,5},{5,4},{6,7},{7,6},{8,9},{9,8},{10,11... | collective-permute-start | bytes 4718600 | tf_op jit(solution)/shard_map/ppermute | solution.py:34
  82.0 8.6 %collective-permute-start.1 = (bf16[2048,384]{1,0:T(8,128)(2,1)}, bf16[2048,384]{1,0:T(8,128)(2,1)}, u32[]{:S(2)}, u32[]{:S(2)}) collective-permute-start(bf16[2048,384]{1,0:T(8,128)(2,1)} %bitcast.58), channel_id=1, source_target_pairs={{0,1},{1,0},{2,3},{3,2},{4,5},{5,4},{6,7},{7,6},{8,9},{9,8},{10,11... | collective-permute-start | bytes 4718600 | tf_op jit(solution)/shard_map/ppermute | solution.py:34
  82.5 13.7 %collective-permute-start.2 = (bf16[384,2048]{1,0:T(8,128)(2,1)}, bf16[384,2048]{1,0:T(8,128)(2,1)}, u32[]{:S(2)}, u32[]{:S(2)}) collective-permute-start(bf16[384,2048]{1,0:T(8,128)(2,1)} %bitcast.55), channel_id=1, source_target_pairs={{0,1},{1,0},{2,3},{3,2},{4,5},{5,4},{6,7},{7,6},{8,9},{9,8},{10,11... | collective-permute-start | bytes 4718600 | tf_op jit(solution)/shard_map/ppermute | solution.py:34
  85.1 5.5 %copy-start.11 = (bf16[1,2048,384]{2,1,0:T(8,128)(2,1)S(1)}, bf16[1,2048,384]{2,1,0:T(8,128)(2,1)}, u32[]{:S(2)}) copy-start(bf16[1,2048,384]{2,1,0:T(8,128)(2,1)} %param.11) | copy-start | bytes 4718596
  90.5 5.6 %copy-start.14 = (f32[512,768]{1,0:T(8,128)}, f32[512,768]{1,0:T(8,128)S(1)}, u32[]{:S(2)}) copy-start(f32[512,768]{1,0:T(8,128)S(1)} %fusion.10) | copy-start | bytes 4718596
  90.6 6.5 %copy-start.9 = (bf16[1,384,2048]{2,1,0:T(8,128)(2,1)S(1)}, bf16[1,384,2048]{2,1,0:T(8,128)(2,1)}, u32[]{:S(2)}) copy-start(bf16[1,384,2048]{2,1,0:T(8,128)(2,1)} %param.12) | copy-start | bytes 4718596
  138.2 58.5 %all-to-all-start.2 = ((bf16[128,4,2048]{2,1,0:T(4,128)(2,1)}), bf16[128,4,2048]{2,1,0:T(4,128)(2,1)}, u32[]{:S(2)}, u32[]{:S(2)}) async-start(bf16[128,4,2048]{2,1,0:T(4,128)(2,1)} %reshape.71), calls=%async_computation.2 | async-start | bytes 4194304 | tf_op jit(solution)/shard_map/all_to_all | solution.py:15
  148.7 4.7 %copy-start.3 = (f32[768,2048]{1,0:T(8,128)}, f32[768,2048]{1,0:T(8,128)S(1)}, u32[]{:S(2)}) copy-start(f32[768,2048]{1,0:T(8,128)S(1)} %fusion.31) | copy-start | bytes 18874372
  148.8 4.7 %copy-start.10 = (bf16[1,384,2048]{2,1,0:T(8,128)(2,1)S(1)}, bf16[1,384,2048]{2,1,0:T(8,128)(2,1)}, u32[]{:S(2)}) copy-start(bf16[1,384,2048]{2,1,0:T(8,128)(2,1)} %param.12) | copy-start | bytes 4718596
  148.8 5.8 %copy-start.15 = (f32[512,768]{1,0:T(8,128)S(1)}, f32[512,768]{1,0:T(8,128)}, u32[]{:S(2)}) copy-start(f32[512,768]{1,0:T(8,128)} %copy-done.14) | copy-start | bytes 4718596
  148.8 6.3 %copy-start.16 = (f32[512,768]{1,0:T(8,128)S(1)}, f32[512,768]{1,0:T(8,128)}, u32[]{:S(2)}) copy-start(f32[512,768]{1,0:T(8,128)} %get-tuple-element.22) | copy-start | bytes 4718596
  153.4 53.5 %collective-permute-start.5 = (f32[384,2048]{1,0:T(8,128)}, f32[384,2048]{1,0:T(8,128)}, u32[]{:S(2)}, u32[]{:S(2)}) collective-permute-start(f32[384,2048]{1,0:T(8,128)} %slice_select_fusion), channel_id=1, source_target_pairs={{0,1},{1,0},{2,3},{3,2},{4,5},{5,4},{6,7},{7,6},{8,9},{9,8},{10,11... | collective-permute-start | bytes 9437192 | tf_op jit(solution)/shard_map/ppermute | solution.py:93
  164.8 48.0 %collective-permute-start.3 = (f32[2048,384]{1,0:T(8,128)}, f32[2048,384]{1,0:T(8,128)}, u32[]{:S(2)}, u32[]{:S(2)}) collective-permute-start(f32[2048,384]{1,0:T(8,128)} %slice_select_fusion.2), channel_id=1, source_target_pairs={{0,1},{1,0},{2,3},{3,2},{4,5},{5,4},{6,7},{7,6},{8,9},{9,8},{10,11... | collective-permute-start | bytes 9437192 | tf_op jit(solution)/shard_map/ppermute | solution.py:93
  196.8 58.1 %all-to-all-start.3 = ((bf16[128,4,2048]{2,1,0:T(4,128)(2,1)}), bf16[128,4,2048]{2,1,0:T(4,128)(2,1)S(1)}, u32[]{:S(2)}, u32[]{:S(2)}) async-start(bf16[128,4,2048]{2,1,0:T(4,128)(2,1)} %reshape.73), calls=%async_computation.3 | async-start | bytes 4194304 | tf_op jit(solution)/shard_map/all_to_all | solution.py:15
  203.2 9.6 %slice-start = ((s8[6291456]{0:T(1024)(128)(4,1)}), s8[4194304]{0:T(1024)(128)(4,1)S(1)}, s32[]{:S(2)}) async-start(s8[6291456]{0:T(1024)(128)(4,1)} %bitcast.46), calls=%async_computation.4 | async-start | bytes 8388608
  206.6 6.2 %slice-start.1 = ((s8[6291456]{0:T(1024)(128)(4,1)}), s8[2097152]{0:T(1024)(128)(4,1)S(1)}, s32[]{:S(2)}) async-start(s8[6291456]{0:T(1024)(128)(4,1)} %bitcast.46), calls=%async_computation.5 | async-start | bytes 4194304
  206.6 10.1 %collective-permute-start.4 = (f32[2048,384]{1,0:T(8,128)S(1)}, f32[2048,384]{1,0:T(8,128)S(1)}, u32[]{:S(2)}, u32[]{:S(2)}) collective-permute-start(f32[2048,384]{1,0:T(8,128)S(1)} %slice_select_fusion.1), channel_id=1, source_target_pairs={{0,1},{1,0},{2,3},{3,2},{4,5},{5,4},{6,7},{7,6},{8,9},{9,8},{10,11... | collective-permute-start | bytes 9437192 | tf_op jit(solution)/shard_map/ppermute | solution.py:93
  207.0 9.7 %slice-start.2 = ((s8[6291456]{0:T(1024)(128)(4,1)}), s8[4194304]{0:T(1024)(128)(4,1)S(1)}, s32[]{:S(2)}) async-start(s8[6291456]{0:T(1024)(128)(4,1)} %bitcast.48), calls=%async_computation.6 | async-start | bytes 8388608
  222.3 37.5 %copy-start.1 = (bf16[128,2048]{1,0:T(8,128)(2,1)S(1)}, bf16[128,2048]{1,0:T(8,128)(2,1)}, u32[]{:S(2)}) copy-start(bf16[128,2048]{1,0:T(8,128)(2,1)} %param.7) | copy-start | bytes 1572868
  (7 other events, 23.5 us)

commit v2 on v1

--- a/solution.py
+++ b/solution.py
@@ -78,7 +78,7 @@
         jnp.dot(dact, wg.T, preferred_element_type=f32)
         + jnp.dot(dupv, wu.T, preferred_element_type=f32)
     ).astype(jnp.bfloat16)
-    pgrad, o_back = lax.optimization_barrier((pack(pgrad, chips), o_back))
+    pgrad, o_back, dact, dupv, hidden = lax.optimization_barrier((pack(pgrad, chips), o_back, dact, dupv, hidden))
     o_back = unpack(o_back)
     p_back = unpack(to_chips(pgrad))
 

time: 261 us -> 256 us (0.981)
  matrix products: 48.3 us -> 44.7 us
    dot_general x1, matrix products: 4.45 us -> 1.83 us  [local(): grad_u = jnp.dot(xrows.T, dupv, preferred_element_type=f32)]
    unnamed x44 -> x46, local copies, waits for them, and re-layouts: 7.24 us -> 5.94 us
  transfers between devices with their start and end apart: 10 -> 10, of which waited for: 5 -> 5; matrix products, arithmetic and copies ran while one was open for 32% -> 33% of each run, Pallas kernels for 0% -> 0%
where the time goes in v2:
time: 256 us; the launch traced here: 255 us
  waiting for transfers between devices  118 us (46%)
  matrix products  44.7 us (17%)
  starting transfers between devices  37 us (14%)
  local copies, waits for them, and re-layouts  32.7 us (13%)
  other arithmetic  21.3 us (8%)
    all_to_all x4, waiting for transfers between devices, to_chips(): return lax.all_to_all(packed, CHIPS, 0, 0, tiled=True)  117 us
    all_to_all x4, starting transfers between devices, to_chips(): return lax.all_to_all(packed, CHIPS, 0, 0, tiled=True)  35.8 us
    reshape x4, local copies, waits for them, and re-layouts, pack(): return rows.reshape(chips, -1, rows.shape[1])  14.6 us
    broadcast_in_dim x3, other arithmetic, local(): return (mixed, d_tokens, d_gate[None], d_up[None], d_down[None])  13.4 us
    reshape x4, local copies, waits for them, and re-layouts, unpack(): return sent.reshape(-1, sent.shape[2])  11.6 us
    dot_general x1, matrix products, local(): dhid = jnp.dot(qrows, wd.T, preferred_element_type=f32)  6.71 us
    unnamed x46, local copies, waits for them, and re-layouts  5.94 us
    dot_general x1, matrix products, local(): upv = jnp.dot(xrows, wu, preferred_element_type=f32)  5.57 us
  transfers between devices with their start and end apart: 10, of which 5 were waited for; matrix products, arithmetic and copies ran while one was open for 33% of the time, Pallas kernels for 0%

profile of v2, /device:TPU:32, one launch (start us, length us, event | category | flops | bytes accessed | tf_op | source)
XLA Modules:
  0.0 254.7 jit_solution(14090730584793007795)
XLA Ops:
  6.4 15.1 %all-to-all-start = ((bf16[128,4,2048]{2,1,0:T(4,128)(2,1)}), bf16[128,4,2048]{2,1,0:T(4,128)(2,1)S(1)}, u32[]{:S(2)}, u32[]{:S(2)}) async-start(bf16[128,4,2048]{2,1,0:T(4,128)(2,1)} %reshape.69), calls=%async_computation | async-start | bytes 4194304 | tf_op jit(solution)/shard_map/all_to_all | solution.py:15
  23.9 4.1 %reshape.68 = bf16[128,4,2048]{2,1,0:T(4,128)(2,1)} reshape(bf16[512,2048]{1,0:T(8,128)(2,1)} %bitcast_convert_fusion) | data formatting | bytes 4194304 | tf_op jit(solution)/shard_map/reshape | solution.py:11
  28.0 47.0 %all-to-all-done = bf16[128,4,2048]{2,1,0:T(4,128)(2,1)S(1)} async-done(((bf16[128,4,2048]{2,1,0:T(4,128)(2,1)}), bf16[128,4,2048]{2,1,0:T(4,128)(2,1)S(1)}, u32[]{:S(2)}, u32[]{:S(2)}) %all-to-all-start) | async-done | bytes 2097184 | tf_op jit(solution)/shard_map/all_to_all | solution.py:15
  75.0 6.9 %all-to-all-start.1 = ((bf16[128,4,2048]{2,1,0:T(4,128)(2,1)}), bf16[128,4,2048]{2,1,0:T(4,128)(2,1)}, u32[]{:S(2)}, u32[]{:S(2)}) async-start(bf16[128,4,2048]{2,1,0:T(4,128)(2,1)} %reshape.68), calls=%async_computation.1 | async-start | bytes 4194304 | tf_op jit(solution)/shard_map/all_to_all | solution.py:15
  82.6 2.5 reshape.70
  85.7 4.8 %fusion.10 = f32[512,768]{1,0:T(8,128)S(1)} fusion(bf16[512,2048]{1,0:T(8,128)(2,1)S(1)} %reshape.70, bf16[2048,384]{1,0:T(8,128)(2,1)} %collective-permute-done, bf16[2048,384]{1,0:T(8,128)(2,1)} %bitcast.62, pred[]{:T(512)S(6)} %eq.62), kind=kOutput, calls=%fused_computation.30 | convolution fusion | flops 1624768512 | bytes 6815745 | tf_op jit(solution)/shard_map/dot_general | solution.py:64
  90.6 5.6 %multiply_convert_fusion.3 = (bf16[512,768]{1,0:T(8,128)(2,1)S(1)}, f32[512,768]{1,0:T(8,128)}) fusion(f32[512,768]{1,0:T(8,128)S(1)} %fusion.10, bf16[512,2048]{1,0:T(8,128)(2,1)S(1)} %reshape.70, bf16[2048,384]{1,0:T(8,128)(2,1)} %collective-permute-done.1, bf16[2048,384]{1,0:T(8,128)(2,1)S(1)} %bitcast.59, pred[]{:T(512)S(6)} %eq.62), kind=kOutput, calls=%fused_computation.21 | convolution fusion | flops 1627127808 | bytes 9175041 | tf_op jit(solution)/shard_map/dot_general | solution.py:65
  97.0 5.2 %convolution_convert_fusion.1 = bf16[512,2048]{1,0:T(8,128)(2,1)} fusion(bf16[512,768]{1,0:T(8,128)(2,1)S(1)} %get-tuple-element.22, bf16[384,2048]{1,0:T(8,128)(2,1)} %collective-permute-done.2, bf16[384,2048]{1,0:T(8,128)(2,1)S(1)} %bitcast.57, pred[]{:T(512)S(6)} %eq.62), kind=kOutput, calls=%fused_computation.9 | convolution fusion | flops 1625817088 | bytes 6029313 | tf_op jit(solution)/shard_map/dot_general | solution.py:69
  102.2 4.1 %reshape.71 = bf16[128,4,2048]{2,1,0:T(4,128)(2,1)} reshape(bf16[512,2048]{1,0:T(8,128)(2,1)} %convolution_convert_fusion.1) | data formatting | bytes 4194304 | tf_op jit(solution)/shard_map/reshape | solution.py:11
  106.3 27.8 %all-to-all-done.1 = bf16[128,4,2048]{2,1,0:T(4,128)(2,1)} async-done(((bf16[128,4,2048]{2,1,0:T(4,128)(2,1)}), bf16[128,4,2048]{2,1,0:T(4,128)(2,1)}, u32[]{:S(2)}, u32[]{:S(2)}) %all-to-all-start.1) | async-done | bytes 2097184 | tf_op jit(solution)/shard_map/all_to_all | solution.py:15
  134.1 6.9 %all-to-all-start.2 = ((bf16[128,4,2048]{2,1,0:T(4,128)(2,1)}), bf16[128,4,2048]{2,1,0:T(4,128)(2,1)}, u32[]{:S(2)}, u32[]{:S(2)}) async-start(bf16[128,4,2048]{2,1,0:T(4,128)(2,1)} %reshape.71), calls=%async_computation.2 | async-start | bytes 4194304 | tf_op jit(solution)/shard_map/all_to_all | solution.py:15
  141.0 4.0 %reshape.72 = bf16[512,2048]{1,0:T(8,128)(2,1)} reshape(bf16[128,4,2048]{2,1,0:T(4,128)(2,1)} %all-to-all-done.1) | data formatting | bytes 4194304 | tf_op jit(solution)/shard_map/reshape | solution.py:19
  145.0 6.7 %multiply_convert_fusion.2 = (bf16[512,768]{1,0:T(8,128)(2,1)S(1)}, bf16[512,768]{1,0:T(8,128)(2,1)S(1)}) fusion(f32[512,768]{1,0:T(8,128)} %copy-done.17, f32[512,768]{1,0:T(8,128)} %get-tuple-element.28, bf16[512,2048]{1,0:T(8,128)(2,1)} %reshape.72, bf16[384,2048]{1,0:T(8,128)(2,1)} %collective-permute-done.2, bf16[384,2048]{1,0:T(8,128)(2,1)} %bitcast.56, ...), kind=kOutput, calls=%fused_computation.20 | convolution fusion | flops 1629880320 | bytes 9961473 | tf_op jit(solution)/shard_map/dot_general | solution.py:74
  151.7 4.2 %fusion.8 = f32[512,2048]{1,0:T(8,128)S(1)} fusion(bf16[512,768]{1,0:T(8,128)(2,1)S(1)} %get-tuple-element.21, bf16[2048,384]{1,0:T(8,128)(2,1)} %collective-permute-done.1, bf16[2048,384]{1,0:T(8,128)(2,1)S(1)} %bitcast.60, pred[]{:T(512)S(6)} %eq.62), kind=kOutput, calls=%fused_computation.28 | convolution fusion | flops 1624768512 | bytes 8126465 | tf_op jit(solution)/shard_map/dot_general | solution.py:79
  155.9 5.1 %add_convert_fusion = bf16[512,2048]{1,0:T(8,128)(2,1)} fusion(f32[512,2048]{1,0:T(8,128)S(1)} %fusion.8, bf16[512,768]{1,0:T(8,128)(2,1)S(1)} %get-tuple-element.20, bf16[2048,384]{1,0:T(8,128)(2,1)} %collective-permute-done, bf16[2048,384]{1,0:T(8,128)(2,1)S(1)} %bitcast.63, pred[]{:T(512)S(6)} %eq.62), kind=kOutput, calls=%fused_computation.1 | convolution fusion | flops 1626865664 | bytes 10223617 | tf_op jit(solution)/shard_map/dot_general | solution.py:78
  161.1 4.1 %reshape.73 = bf16[128,4,2048]{2,1,0:T(4,128)(2,1)} reshape(bf16[512,2048]{1,0:T(8,128)(2,1)} %add_convert_fusion) | data formatting | bytes 4194304 | tf_op jit(solution)/shard_map/reshape | solution.py:11
  165.2 27.5 %all-to-all-done.2 = bf16[128,4,2048]{2,1,0:T(4,128)(2,1)} async-done(((bf16[128,4,2048]{2,1,0:T(4,128)(2,1)}), bf16[128,4,2048]{2,1,0:T(4,128)(2,1)}, u32[]{:S(2)}, u32[]{:S(2)}) %all-to-all-start.2) | async-done | bytes 2097184 | tf_op jit(solution)/shard_map/all_to_all | solution.py:15
  192.7 6.9 %all-to-all-start.3 = ((bf16[128,4,2048]{2,1,0:T(4,128)(2,1)}), bf16[128,4,2048]{2,1,0:T(4,128)(2,1)}, u32[]{:S(2)}, u32[]{:S(2)}) async-start(bf16[128,4,2048]{2,1,0:T(4,128)(2,1)} %reshape.73), calls=%async_computation.3 | async-start | bytes 4194304 | tf_op jit(solution)/shard_map/all_to_all | solution.py:15
  199.6 3.7 %fusion.31 = f32[768,2048]{1,0:T(8,128)S(1)} fusion(bf16[512,768]{1,0:T(8,128)(2,1)} %copy-done.6, bf16[512,2048]{1,0:T(8,128)(2,1)} %reshape.72), kind=kOutput, calls=%fused_computation.59 | convolution fusion | flops 1610612736 | bytes 9175040 | tf_op jit(solution)/shard_map/dot_general | solution.py:87
  222.3 5.8 %fusion.2 = bf16[1,384,2048]{2,1,0:T(8,128)(2,1)} fusion(f32[384,2048]{1,0:T(8,128)} %collective-permute-done.5, f32[768,2048]{1,0:T(8,128)} %copy-done.4, pred[]{:T(512)S(6)} %eq.62), kind=kLoop, calls=%fused_computation.18 | loop fusion | flops 2359296 | bytes 11010049 | tf_op jit(solution)/shard_map/broadcast_in_dim | solution.py:101
  228.2 3.9 %fusion = bf16[1,2048,384]{2,1,0:T(8,128)(2,1)} fusion(f32[2048,384]{1,0:T(8,128)} %collective-permute-done.3, f32[2048,768]{1,0:T(8,128)S(1)} %bitcast.49, pred[]{:T(512)S(6)} %eq.62), kind=kLoop, calls=%fused_computation.16 | loop fusion | flops 2359296 | bytes 11010049 | tf_op jit(solution)/shard_map/broadcast_in_dim | solution.py:101
  232.1 3.8 %fusion.1 = bf16[1,2048,384]{2,1,0:T(8,128)(2,1)} fusion(f32[2048,384]{1,0:T(8,128)} %collective-permute-done.4, f32[2048,768]{1,0:T(8,128)S(1)} %bitcast.47, pred[]{:T(512)S(6)} %eq.62), kind=kLoop, calls=%fused_computation.17 | loop fusion | flops 2359296 | bytes 11010049 | tf_op jit(solution)/shard_map/broadcast_in_dim | solution.py:101
  235.8 15.1 %all-to-all-done.3 = bf16[128,4,2048]{2,1,0:T(4,128)(2,1)} async-done(((bf16[128,4,2048]{2,1,0:T(4,128)(2,1)}), bf16[128,4,2048]{2,1,0:T(4,128)(2,1)}, u32[]{:S(2)}, u32[]{:S(2)}) %all-to-all-start.3) | async-done | bytes 2097184 | tf_op jit(solution)/shard_map/all_to_all | solution.py:15
  250.9 2.5 reshape.75
  (87 shorter events, 30.4 us)
Async XLA Ops:
  6.4 15.2 %copy-start.11 = (bf16[128,2048]{1,0:T(8,128)(2,1)S(1)}, bf16[128,2048]{1,0:T(8,128)(2,1)}, u32[]{:S(2)}) copy-start(bf16[128,2048]{1,0:T(8,128)(2,1)} %param.13) | copy-start | bytes 1572868
  6.4 15.3 %copy-start.12 = (s32[128,2]{0,1:T(2,128)S(1)}, s32[128,2]{0,1:T(2,128)}, u32[]{:S(2)}) copy-start(s32[128,2]{0,1:T(2,128)} %param.9) | copy-start | bytes 3076
  6.4 68.6 %all-to-all-start = ((bf16[128,4,2048]{2,1,0:T(4,128)(2,1)}), bf16[128,4,2048]{2,1,0:T(4,128)(2,1)S(1)}, u32[]{:S(2)}, u32[]{:S(2)}) async-start(bf16[128,4,2048]{2,1,0:T(4,128)(2,1)} %reshape.69), calls=%async_computation | async-start | bytes 4194304 | tf_op jit(solution)/shard_map/all_to_all | solution.py:15
  75.0 7.6 %copy-start.5 = (bf16[128,4,2048]{2,1,0:T(4,128)(2,1)}, bf16[128,4,2048]{2,1,0:T(4,128)(2,1)S(1)}, u32[]{:S(2)}) copy-start(bf16[128,4,2048]{2,1,0:T(4,128)(2,1)S(1)} %all-to-all-done) | copy-start | bytes 6291460
  75.0 59.1 %all-to-all-start.1 = ((bf16[128,4,2048]{2,1,0:T(4,128)(2,1)}), bf16[128,4,2048]{2,1,0:T(4,128)(2,1)}, u32[]{:S(2)}, u32[]{:S(2)}) async-start(bf16[128,4,2048]{2,1,0:T(4,128)(2,1)} %reshape.68), calls=%async_computation.1 | async-start | bytes 4194304 | tf_op jit(solution)/shard_map/all_to_all | solution.py:15
  81.9 3.8 %collective-permute-start = (bf16[2048,384]{1,0:T(8,128)(2,1)}, bf16[2048,384]{1,0:T(8,128)(2,1)}, u32[]{:S(2)}, u32[]{:S(2)}) collective-permute-start(bf16[2048,384]{1,0:T(8,128)(2,1)} %bitcast.61), channel_id=1, source_target_pairs={{0,1},{1,0},{2,3},{3,2},{4,5},{5,4},{6,7},{7,6},{8,9},{9,8},{10,11... | collective-permute-start | bytes 4718600 | tf_op jit(solution)/shard_map/ppermute | solution.py:34
  82.0 8.6 %collective-permute-start.1 = (bf16[2048,384]{1,0:T(8,128)(2,1)}, bf16[2048,384]{1,0:T(8,128)(2,1)}, u32[]{:S(2)}, u32[]{:S(2)}) collective-permute-start(bf16[2048,384]{1,0:T(8,128)(2,1)} %bitcast.58), channel_id=1, source_target_pairs={{0,1},{1,0},{2,3},{3,2},{4,5},{5,4},{6,7},{7,6},{8,9},{9,8},{10,11... | collective-permute-start | bytes 4718600 | tf_op jit(solution)/shard_map/ppermute | solution.py:34
  82.5 13.7 %collective-permute-start.2 = (bf16[384,2048]{1,0:T(8,128)(2,1)}, bf16[384,2048]{1,0:T(8,128)(2,1)}, u32[]{:S(2)}, u32[]{:S(2)}) collective-permute-start(bf16[384,2048]{1,0:T(8,128)(2,1)} %bitcast.55), channel_id=1, source_target_pairs={{0,1},{1,0},{2,3},{3,2},{4,5},{5,4},{6,7},{7,6},{8,9},{9,8},{10,11... | collective-permute-start | bytes 4718600 | tf_op jit(solution)/shard_map/ppermute | solution.py:34
  85.1 5.4 %copy-start.14 = (bf16[1,2048,384]{2,1,0:T(8,128)(2,1)S(1)}, bf16[1,2048,384]{2,1,0:T(8,128)(2,1)}, u32[]{:S(2)}) copy-start(bf16[1,2048,384]{2,1,0:T(8,128)(2,1)} %param.11) | copy-start | bytes 4718596
  90.5 5.6 %copy-start.17 = (f32[512,768]{1,0:T(8,128)}, f32[512,768]{1,0:T(8,128)S(1)}, u32[]{:S(2)}) copy-start(f32[512,768]{1,0:T(8,128)S(1)} %fusion.10) | copy-start | bytes 4718596
  90.5 6.5 %copy-start.13 = (bf16[1,384,2048]{2,1,0:T(8,128)(2,1)S(1)}, bf16[1,384,2048]{2,1,0:T(8,128)(2,1)}, u32[]{:S(2)}) copy-start(bf16[1,384,2048]{2,1,0:T(8,128)(2,1)} %param.12) | copy-start | bytes 4718596
  134.1 58.6 %all-to-all-start.2 = ((bf16[128,4,2048]{2,1,0:T(4,128)(2,1)}), bf16[128,4,2048]{2,1,0:T(4,128)(2,1)}, u32[]{:S(2)}, u32[]{:S(2)}) async-start(bf16[128,4,2048]{2,1,0:T(4,128)(2,1)} %reshape.71), calls=%async_computation.2 | async-start | bytes 4194304 | tf_op jit(solution)/shard_map/all_to_all | solution.py:15
  145.0 6.7 %copy-start.15 = (bf16[1,2048,384]{2,1,0:T(8,128)(2,1)S(1)}, bf16[1,2048,384]{2,1,0:T(8,128)(2,1)}, u32[]{:S(2)}) copy-start(bf16[1,2048,384]{2,1,0:T(8,128)(2,1)} %param.11) | copy-start | bytes 4718596
  151.7 4.2 %copy-start.7 = (bf16[512,768]{1,0:T(8,128)(2,1)}, bf16[512,768]{1,0:T(8,128)(2,1)S(1)}, u32[]{:S(2)}) copy-start(bf16[512,768]{1,0:T(8,128)(2,1)S(1)} %get-tuple-element.21) | copy-start | bytes 2359300
  151.7 4.2 %copy-start.9 = (bf16[512,768]{1,0:T(8,128)(2,1)}, bf16[512,768]{1,0:T(8,128)(2,1)S(1)}, u32[]{:S(2)}) copy-start(bf16[512,768]{1,0:T(8,128)(2,1)S(1)} %get-tuple-element.20) | copy-start | bytes 2359300
  151.7 4.2 %copy-start.16 = (bf16[1,2048,384]{2,1,0:T(8,128)(2,1)S(1)}, bf16[1,2048,384]{2,1,0:T(8,128)(2,1)}, u32[]{:S(2)}) copy-start(bf16[1,2048,384]{2,1,0:T(8,128)(2,1)} %param.10) | copy-start | bytes 4718596
  192.7 58.3 %all-to-all-start.3 = ((bf16[128,4,2048]{2,1,0:T(4,128)(2,1)}), bf16[128,4,2048]{2,1,0:T(4,128)(2,1)}, u32[]{:S(2)}, u32[]{:S(2)}) async-start(bf16[128,4,2048]{2,1,0:T(4,128)(2,1)} %reshape.73), calls=%async_computation.3 | async-start | bytes 4194304 | tf_op jit(solution)/shard_map/all_to_all | solution.py:15
  206.8 15.5 %collective-permute-start.5 = (f32[384,2048]{1,0:T(8,128)}, f32[384,2048]{1,0:T(8,128)}, u32[]{:S(2)}, u32[]{:S(2)}) collective-permute-start(f32[384,2048]{1,0:T(8,128)} %slice_select_fusion), channel_id=1, source_target_pairs={{0,1},{1,0},{2,3},{3,2},{4,5},{5,4},{6,7},{7,6},{8,9},{9,8},{10,11... | collective-permute-start | bytes 9437192 | tf_op jit(solution)/shard_map/ppermute | solution.py:93
  212.3 15.9 %collective-permute-start.3 = (f32[2048,384]{1,0:T(8,128)}, f32[2048,384]{1,0:T(8,128)}, u32[]{:S(2)}, u32[]{:S(2)}) collective-permute-start(f32[2048,384]{1,0:T(8,128)} %slice_select_fusion.2), channel_id=1, source_target_pairs={{0,1},{1,0},{2,3},{3,2},{4,5},{5,4},{6,7},{7,6},{8,9},{9,8},{10,11... | collective-permute-start | bytes 9437192 | tf_op jit(solution)/shard_map/ppermute | solution.py:93
  218.2 13.9 %collective-permute-start.4 = (f32[2048,384]{1,0:T(8,128)}, f32[2048,384]{1,0:T(8,128)}, u32[]{:S(2)}, u32[]{:S(2)}) collective-permute-start(f32[2048,384]{1,0:T(8,128)} %slice_select_fusion.1), channel_id=1, source_target_pairs={{0,1},{1,0},{2,3},{3,2},{4,5},{5,4},{6,7},{7,6},{8,9},{9,8},{10,11... | collective-permute-start | bytes 9437192 | tf_op jit(solution)/shard_map/ppermute | solution.py:93
  220.7 7.5 %slice-start.2 = ((s8[6291456]{0:T(1024)(128)(4,1)}), s8[4194304]{0:T(1024)(128)(4,1)S(1)}, s32[]{:S(2)}) async-start(s8[6291456]{0:T(1024)(128)(4,1)} %bitcast.48), calls=%async_computation.6 | async-start | bytes 8388608
  222.3 5.8 %slice-start.3 = ((s8[6291456]{0:T(1024)(128)(4,1)}), s8[2097152]{0:T(1024)(128)(4,1)S(1)}, s32[]{:S(2)}) async-start(s8[6291456]{0:T(1024)(128)(4,1)} %bitcast.48), calls=%async_computation.7 | async-start | bytes 4194304
  222.3 9.7 %slice-start = ((s8[6291456]{0:T(1024)(128)(4,1)}), s8[4194304]{0:T(1024)(128)(4,1)S(1)}, s32[]{:S(2)}) async-start(s8[6291456]{0:T(1024)(128)(4,1)} %bitcast.46), calls=%async_computation.4 | async-start | bytes 8388608
  232.1 22.6 %copy-start.1 = (bf16[128,2048]{1,0:T(8,128)(2,1)S(1)}, bf16[128,2048]{1,0:T(8,128)(2,1)}, u32[]{:S(2)}) copy-start(bf16[128,2048]{1,0:T(8,128)(2,1)} %param.7) | copy-start | bytes 1572868
  (8 other events, 25.8 us)

commit v3 on v2

--- a/solution.py
+++ b/solution.py
@@ -82,18 +82,22 @@
     o_back = unpack(o_back)
     p_back = unpack(to_chips(pgrad))
 
-    grad_g = jnp.dot(xrows.T, dact, preferred_element_type=f32)
-    grad_u = jnp.dot(xrows.T, dupv, preferred_element_type=f32)
-    grad_d = jnp.dot(hidden.T, qrows, preferred_element_type=f32)
-    g_lo, g_hi = grad_g[:, :half], grad_g[:, half:]
-    u_lo, u_hi = grad_u[:, :half], grad_u[:, half:]
-    d_lo, d_hi = grad_d[:half], grad_d[half:]
-    mine = (jnp.where(first, g_lo, g_hi), jnp.where(first, u_lo, u_hi), jnp.where(first, d_lo, d_hi))
-    other = (jnp.where(first, g_hi, g_lo), jnp.where(first, u_hi, u_lo), jnp.where(first, d_hi, d_lo))
+    def halves(value):
+        lo, hi = value[:, :half], value[:, half:]
+        return jnp.where(first, lo, hi), jnp.where(first, hi, lo)
+
+    dact_m, dact_o = halves(dact)
+    dupv_m, dupv_o = halves(dupv)
+    hid_m, hid_o = halves(hidden)
+    other = (
+        jnp.dot(xrows.T, dact_o, preferred_element_type=f32),
+        jnp.dot(xrows.T, dupv_o, preferred_element_type=f32),
+        jnp.dot(hid_o.T, qrows, preferred_element_type=f32),
+    )
     came = lax.ppermute(other, "core", swap)
-    d_gate = (mine[0] + came[0]).astype(jnp.bfloat16)
-    d_up = (mine[1] + came[1]).astype(jnp.bfloat16)
-    d_down = (mine[2] + came[2]).astype(jnp.bfloat16)
+    d_gate = (jnp.dot(xrows.T, dact_m, preferred_element_type=f32) + came[0]).astype(jnp.bfloat16)
+    d_up = (jnp.dot(xrows.T, dupv_m, preferred_element_type=f32) + came[1]).astype(jnp.bfloat16)
+    d_down = (jnp.dot(hid_m.T, qrows, preferred_element_type=f32) + came[2]).astype(jnp.bfloat16)
 
     o_k = jnp.einsum("kts,sw->ktw", pick, o_back, preferred_element_type=f32)
     mixed = (gates.reshape(tok_rows, top).T[:, :, None] * o_k).sum(0).astype(jnp.bfloat16)

time: 256 us -> 262 us (1.023)
  other arithmetic: 21.3 us -> 1.35 us
  matrix products: 44.7 us -> 63.5 us
  waiting for transfers between devices: 118 us -> 128 us
  local copies, waits for them, and re-layouts: 32.7 us -> 29.8 us
    dot_general x3 -> x6, matrix products: 7.33 us -> 24.3 us  [the longest x1 4.41 us: local(): jnp.dot(xrows.T, dact_m, preferred_element_type=f32) + came[0]]
    broadcast_in_dim x3 -> x0, other arithmetic: 13.4 us -> none  [local(): return (mixed, d_tokens, d_gate[None], d_up[None], d_down[None])]
    all_to_all x4, waiting for transfers between devices: 117 us -> 128 us  [to_chips(): return lax.all_to_all(packed, CHIPS, 0, 0, tiled=True)]
    select_n x3 -> x0, other arithmetic: 6.51 us -> none  [the longest x1 2.39 us: local(): jnp.where(first, d_hi, d_lo)]
    unnamed x46 -> x38, local copies, waits for them, and re-layouts: 5.94 us -> 1.63 us
  transfers between devices with their start and end apart: 10 -> 10, of which waited for: 5 -> 5; matrix products, arithmetic and copies ran while one was open for 33% -> 31% of each run, Pallas kernels for 0% -> 0%
where the time goes in v3:
time: 262 us; the launch traced here: 261 us
  waiting for transfers between devices  128 us (49%)
  matrix products  63.5 us (24%)
  starting transfers between devices  37 us (14%)
  local copies, waits for them, and re-layouts  29.8 us (11%)
    all_to_all x4, waiting for transfers between devices, to_chips(): return lax.all_to_all(packed, CHIPS, 0, 0, tiled=True)  128 us
    all_to_all x4, starting transfers between devices, to_chips(): return lax.all_to_all(packed, CHIPS, 0, 0, tiled=True)  35.8 us
    reshape x4, local copies, waits for them, and re-layouts, pack(): return rows.reshape(chips, -1, rows.shape[1])  14.6 us
    reshape x4, local copies, waits for them, and re-layouts, unpack(): return sent.reshape(-1, sent.shape[2])  13 us
    dot_general x1, matrix products, local(): dhid = jnp.dot(qrows, wd.T, preferred_element_type=f32)  6.71 us
    dot_general x1, matrix products, local(): upv = jnp.dot(xrows, wu, preferred_element_type=f32)  5.57 us
    dot_general x1, matrix products, local(): outv = jnp.dot(hidden, wd, preferred_element_type=f32).astype(jnp.bfloat16)  5.28 us
  transfers between devices with their start and end apart: 10, of which 5 were waited for; matrix products, arithmetic and copies ran while one was open for 31% of the time, Pallas kernels for 0%

profile of v3, /device:TPU:32, one launch (start us, length us, event | category | flops | bytes accessed | tf_op | source)
XLA Modules:
  0.0 261.2 jit_solution(7117589049462220410)
XLA Ops:
  7.1 15.1 %all-to-all-start = ((bf16[128,4,2048]{2,1,0:T(4,128)(2,1)}), bf16[128,4,2048]{2,1,0:T(4,128)(2,1)S(1)}, u32[]{:S(2)}, u32[]{:S(2)}) async-start(bf16[128,4,2048]{2,1,0:T(4,128)(2,1)} %reshape.69), calls=%async_computation | async-start | bytes 4194304 | tf_op jit(solution)/shard_map/all_to_all | solution.py:15
  24.5 4.1 %reshape.68 = bf16[128,4,2048]{2,1,0:T(4,128)(2,1)} reshape(bf16[512,2048]{1,0:T(8,128)(2,1)} %bitcast_convert_fusion) | data formatting | bytes 4194304 | tf_op jit(solution)/shard_map/reshape | solution.py:11
  28.6 47.1 %all-to-all-done = bf16[128,4,2048]{2,1,0:T(4,128)(2,1)S(1)} async-done(((bf16[128,4,2048]{2,1,0:T(4,128)(2,1)}), bf16[128,4,2048]{2,1,0:T(4,128)(2,1)S(1)}, u32[]{:S(2)}, u32[]{:S(2)}) %all-to-all-start) | async-done | bytes 2097184 | tf_op jit(solution)/shard_map/all_to_all | solution.py:15
  75.7 6.9 %all-to-all-start.1 = ((bf16[128,4,2048]{2,1,0:T(4,128)(2,1)}), bf16[128,4,2048]{2,1,0:T(4,128)(2,1)}, u32[]{:S(2)}, u32[]{:S(2)}) async-start(bf16[128,4,2048]{2,1,0:T(4,128)(2,1)} %reshape.68), calls=%async_computation.1 | async-start | bytes 4194304 | tf_op jit(solution)/shard_map/all_to_all | solution.py:15
  86.4 4.7 %fusion.10 = f32[512,768]{1,0:T(8,128)S(1)} fusion(bf16[512,2048]{1,0:T(8,128)(2,1)S(1)} %reshape.70, bf16[2048,384]{1,0:T(8,128)(2,1)} %collective-permute-done, bf16[2048,384]{1,0:T(8,128)(2,1)} %bitcast.58, pred[]{:T(512)S(6)} %eq.62), kind=kOutput, calls=%fused_computation.27 | convolution fusion | flops 1624768512 | bytes 6815745 | tf_op jit(solution)/shard_map/dot_general | solution.py:64
  91.2 5.6 %multiply_convert_fusion.3 = (bf16[512,768]{1,0:T(8,128)(2,1)S(1)}, f32[512,768]{1,0:T(8,128)}) fusion(f32[512,768]{1,0:T(8,128)S(1)} %fusion.10, bf16[512,2048]{1,0:T(8,128)(2,1)S(1)} %reshape.70, bf16[2048,384]{1,0:T(8,128)(2,1)} %collective-permute-done.1, bf16[2048,384]{1,0:T(8,128)(2,1)S(1)} %bitcast.55, pred[]{:T(512)S(6)} %eq.62), kind=kOutput, calls=%fused_computation.18 | convolution fusion | flops 1627127808 | bytes 9175041 | tf_op jit(solution)/shard_map/dot_general | solution.py:65
  96.8 5.3 %convolution_convert_fusion.1 = bf16[512,2048]{1,0:T(8,128)(2,1)} fusion(bf16[512,768]{1,0:T(8,128)(2,1)S(1)} %get-tuple-element.22, bf16[384,2048]{1,0:T(8,128)(2,1)} %collective-permute-done.2, bf16[384,2048]{1,0:T(8,128)(2,1)S(1)} %bitcast.53, pred[]{:T(512)S(6)} %eq.62), kind=kOutput, calls=%fused_computation.9 | convolution fusion | flops 1625817088 | bytes 6029313 | tf_op jit(solution)/shard_map/dot_general | solution.py:69
  102.1 4.1 %reshape.71 = bf16[128,4,2048]{2,1,0:T(4,128)(2,1)} reshape(bf16[512,2048]{1,0:T(8,128)(2,1)} %convolution_convert_fusion.1) | data formatting | bytes 4194304 | tf_op jit(solution)/shard_map/reshape | solution.py:11
  106.2 28.6 %all-to-all-done.1 = bf16[128,4,2048]{2,1,0:T(4,128)(2,1)} async-done(((bf16[128,4,2048]{2,1,0:T(4,128)(2,1)}), bf16[128,4,2048]{2,1,0:T(4,128)(2,1)}, u32[]{:S(2)}, u32[]{:S(2)}) %all-to-all-start.1) | async-done | bytes 2097184 | tf_op jit(solution)/shard_map/all_to_all | solution.py:15
  134.8 6.9 %all-to-all-start.2 = ((bf16[128,4,2048]{2,1,0:T(4,128)(2,1)}), bf16[128,4,2048]{2,1,0:T(4,128)(2,1)}, u32[]{:S(2)}, u32[]{:S(2)}) async-start(bf16[128,4,2048]{2,1,0:T(4,128)(2,1)} %reshape.71), calls=%async_computation.2 | async-start | bytes 4194304 | tf_op jit(solution)/shard_map/all_to_all | solution.py:15
  141.7 3.9 %reshape.72 = bf16[512,2048]{1,0:T(8,128)(2,1)} reshape(bf16[128,4,2048]{2,1,0:T(4,128)(2,1)} %all-to-all-done.1) | data formatting | bytes 4194304 | tf_op jit(solution)/shard_map/reshape | solution.py:19
  145.6 6.7 %multiply_convert_fusion.2 = (bf16[512,768]{1,0:T(8,128)(2,1)S(1)}, bf16[512,768]{1,0:T(8,128)(2,1)S(1)}) fusion(f32[512,768]{1,0:T(8,128)} %copy-done.17, f32[512,768]{1,0:T(8,128)} %get-tuple-element.28, bf16[512,2048]{1,0:T(8,128)(2,1)} %reshape.72, bf16[384,2048]{1,0:T(8,128)(2,1)} %collective-permute-done.2, bf16[384,2048]{1,0:T(8,128)(2,1)} %bitcast.52, ...), kind=kOutput, calls=%fused_computation.17 | convolution fusion | flops 1629880320 | bytes 9961473 | tf_op jit(solution)/shard_map/dot_general | solution.py:74
  152.4 4.2 %fusion.8 = f32[512,2048]{1,0:T(8,128)S(1)} fusion(bf16[512,768]{1,0:T(8,128)(2,1)S(1)} %get-tuple-element.21, bf16[2048,384]{1,0:T(8,128)(2,1)} %collective-permute-done.1, bf16[2048,384]{1,0:T(8,128)(2,1)S(1)} %bitcast.56, pred[]{:T(512)S(6)} %eq.62), kind=kOutput, calls=%fused_computation.25 | convolution fusion | flops 1624768512 | bytes 8126465 | tf_op jit(solution)/shard_map/dot_general | solution.py:79
  156.6 5.2 %add_convert_fusion = bf16[512,2048]{1,0:T(8,128)(2,1)} fusion(f32[512,2048]{1,0:T(8,128)S(1)} %fusion.8, bf16[512,768]{1,0:T(8,128)(2,1)S(1)} %get-tuple-element.20, bf16[2048,384]{1,0:T(8,128)(2,1)} %collective-permute-done, bf16[2048,384]{1,0:T(8,128)(2,1)S(1)} %bitcast.59, pred[]{:T(512)S(6)} %eq.62), kind=kOutput, calls=%fused_computation.1 | convolution fusion | flops 1626865664 | bytes 10223617 | tf_op jit(solution)/shard_map/dot_general | solution.py:78
  161.8 4.1 %reshape.73 = bf16[128,4,2048]{2,1,0:T(4,128)(2,1)} reshape(bf16[512,2048]{1,0:T(8,128)(2,1)} %add_convert_fusion) | data formatting | bytes 4194304 | tf_op jit(solution)/shard_map/reshape | solution.py:11
  165.9 27.4 %all-to-all-done.2 = bf16[128,4,2048]{2,1,0:T(4,128)(2,1)} async-done(((bf16[128,4,2048]{2,1,0:T(4,128)(2,1)}), bf16[128,4,2048]{2,1,0:T(4,128)(2,1)}, u32[]{:S(2)}, u32[]{:S(2)}) %all-to-all-start.2) | async-done | bytes 2097184 | tf_op jit(solution)/shard_map/all_to_all | solution.py:15
  193.4 4.2 %fusion.12 = f32[384,2048]{1,0:T(8,128)} fusion(bf16[512,2048]{1,0:T(8,128)(2,1)} %reshape.72, pred[]{:T(512)S(6)} %eq.62, bf16[512,768]{1,0:T(8,128)(2,1)S(1)} %get-tuple-element.22), kind=kOutput, calls=%fused_computation.31 | convolution fusion | flops 805502976 | bytes 6029313 | tf_op jit(solution)/shard_map/dot_general | solution.py:95
  197.6 6.9 %all-to-all-start.3 = ((bf16[128,4,2048]{2,1,0:T(4,128)(2,1)}), bf16[128,4,2048]{2,1,0:T(4,128)(2,1)}, u32[]{:S(2)}, u32[]{:S(2)}) async-start(bf16[128,4,2048]{2,1,0:T(4,128)(2,1)} %reshape.73), calls=%async_computation.3 | async-start | bytes 4194304 | tf_op jit(solution)/shard_map/all_to_all | solution.py:15
  204.6 4.2 %fusion.18 = f32[2048,384]{1,0:T(8,128)} fusion(bf16[512,2048]{1,0:T(8,128)(2,1)S(1)} %reshape.70, pred[]{:T(512)S(6)} %eq.62, bf16[512,768]{1,0:T(8,128)(2,1)} %copy-done.9), kind=kOutput, calls=%fused_computation.37 | convolution fusion | flops 805502976 | bytes 6029313 | tf_op jit(solution)/shard_map/dot_general | solution.py:93
  212.2 4.0 %reshape.77 = bf16[512,2048,1]{1,0,2:T(8,128)(2,1)} reshape(bf16[128,4,2048]{2,1,0:T(4,128)(2,1)} %all-to-all-done.2) | data formatting | bytes 4194304 | tf_op jit(solution)/shard_map/reshape | solution.py:19
  219.7 4.2 %fusion.2 = bf16[1,384,2048]{2,1,0:T(8,128)(2,1)} fusion(f32[384,2048]{1,0:T(8,128)} %collective-permute-done.5, bf16[512,2048]{1,0:T(8,128)(2,1)S(1)} %copy-done.2, pred[]{:T(512)S(6)} %eq.62, bf16[512,768]{1,0:T(8,128)(2,1)S(1)} %get-tuple-element.22), kind=kOutput, calls=%fused_computation.13 | convolution fusion | flops 807075840 | bytes 7602177 | tf_op jit(solution)/shard_map/dot_general | solution.py:100
  223.8 4.4 %fusion = bf16[1,2048,384]{2,1,0:T(8,128)(2,1)} fusion(f32[2048,384]{1,0:T(8,128)} %collective-permute-done.3, bf16[512,2048]{1,0:T(8,128)(2,1)S(1)} %reshape.70, pred[]{:T(512)S(6)} %eq.62, bf16[512,768]{1,0:T(8,128)(2,1)S(1)} %copy-done.10), kind=kOutput, calls=%fused_computation.11 | convolution fusion | flops 807075840 | bytes 7602177 | tf_op jit(solution)/shard_map/dot_general | solution.py:98
  228.2 4.3 %fusion.1 = bf16[1,2048,384]{2,1,0:T(8,128)(2,1)} fusion(f32[2048,384]{1,0:T(8,128)} %collective-permute-done.4, bf16[512,2048]{1,0:T(8,128)(2,1)S(1)} %reshape.70, pred[]{:T(512)S(6)} %eq.62, bf16[512,768]{1,0:T(8,128)(2,1)S(1)} %copy-done.8), kind=kOutput, calls=%fused_computation.12 | convolution fusion | flops 807075840 | bytes 7602177 | tf_op jit(solution)/shard_map/dot_general | solution.py:99
  232.6 24.7 %all-to-all-done.3 = bf16[128,4,2048]{2,1,0:T(4,128)(2,1)} async-done(((bf16[128,4,2048]{2,1,0:T(4,128)(2,1)}), bf16[128,4,2048]{2,1,0:T(4,128)(2,1)}, u32[]{:S(2)}, u32[]{:S(2)}) %all-to-all-start.3) | async-done | bytes 2097184 | tf_op jit(solution)/shard_map/all_to_all | solution.py:15
  (74 shorter events, 23.3 us)
Async XLA Ops:
  7.1 15.2 %copy-start.11 = (bf16[128,2048]{1,0:T(8,128)(2,1)S(1)}, bf16[128,2048]{1,0:T(8,128)(2,1)}, u32[]{:S(2)}) copy-start(bf16[128,2048]{1,0:T(8,128)(2,1)} %param.13) | copy-start | bytes 1572868
  7.1 15.3 %copy-start.12 = (s32[128,2]{0,1:T(2,128)S(1)}, s32[128,2]{0,1:T(2,128)}, u32[]{:S(2)}) copy-start(s32[128,2]{0,1:T(2,128)} %param.9) | copy-start | bytes 3076
  7.1 68.6 %all-to-all-start = ((bf16[128,4,2048]{2,1,0:T(4,128)(2,1)}), bf16[128,4,2048]{2,1,0:T(4,128)(2,1)S(1)}, u32[]{:S(2)}, u32[]{:S(2)}) async-start(bf16[128,4,2048]{2,1,0:T(4,128)(2,1)} %reshape.69), calls=%async_computation | async-start | bytes 4194304 | tf_op jit(solution)/shard_map/all_to_all | solution.py:15
  75.7 6.9 %copy-start.3 = (bf16[128,4,2048]{2,1,0:T(4,128)(2,1)}, bf16[128,4,2048]{2,1,0:T(4,128)(2,1)S(1)}, u32[]{:S(2)}) copy-start(bf16[128,4,2048]{2,1,0:T(4,128)(2,1)S(1)} %all-to-all-done) | copy-start | bytes 6291460
  75.7 59.1 %all-to-all-start.1 = ((bf16[128,4,2048]{2,1,0:T(4,128)(2,1)}), bf16[128,4,2048]{2,1,0:T(4,128)(2,1)}, u32[]{:S(2)}, u32[]{:S(2)}) async-start(bf16[128,4,2048]{2,1,0:T(4,128)(2,1)} %reshape.68), calls=%async_computation.1 | async-start | bytes 4194304 | tf_op jit(solution)/shard_map/all_to_all | solution.py:15
  82.6 3.8 %collective-permute-start = (bf16[2048,384]{1,0:T(8,128)(2,1)}, bf16[2048,384]{1,0:T(8,128)(2,1)}, u32[]{:S(2)}, u32[]{:S(2)}) collective-permute-start(bf16[2048,384]{1,0:T(8,128)(2,1)} %bitcast.57), channel_id=1, source_target_pairs={{0,1},{1,0},{2,3},{3,2},{4,5},{5,4},{6,7},{7,6},{8,9},{9,8},{10,11... | collective-permute-start | bytes 4718600 | tf_op jit(solution)/shard_map/ppermute | solution.py:34
  82.7 8.5 %collective-permute-start.1 = (bf16[2048,384]{1,0:T(8,128)(2,1)}, bf16[2048,384]{1,0:T(8,128)(2,1)}, u32[]{:S(2)}, u32[]{:S(2)}) collective-permute-start(bf16[2048,384]{1,0:T(8,128)(2,1)} %bitcast.54), channel_id=1, source_target_pairs={{0,1},{1,0},{2,3},{3,2},{4,5},{5,4},{6,7},{7,6},{8,9},{9,8},{10,11... | collective-permute-start | bytes 4718600 | tf_op jit(solution)/shard_map/ppermute | solution.py:34
  83.2 13.6 %collective-permute-start.2 = (bf16[384,2048]{1,0:T(8,128)(2,1)}, bf16[384,2048]{1,0:T(8,128)(2,1)}, u32[]{:S(2)}, u32[]{:S(2)}) collective-permute-start(bf16[384,2048]{1,0:T(8,128)(2,1)} %bitcast.51), channel_id=1, source_target_pairs={{0,1},{1,0},{2,3},{3,2},{4,5},{5,4},{6,7},{7,6},{8,9},{9,8},{10,11... | collective-permute-start | bytes 4718600 | tf_op jit(solution)/shard_map/ppermute | solution.py:34
  85.8 5.4 %copy-start.14 = (bf16[1,2048,384]{2,1,0:T(8,128)(2,1)S(1)}, bf16[1,2048,384]{2,1,0:T(8,128)(2,1)}, u32[]{:S(2)}) copy-start(bf16[1,2048,384]{2,1,0:T(8,128)(2,1)} %param.11) | copy-start | bytes 4718596
  91.2 5.6 %copy-start.17 = (f32[512,768]{1,0:T(8,128)}, f32[512,768]{1,0:T(8,128)S(1)}, u32[]{:S(2)}) copy-start(f32[512,768]{1,0:T(8,128)S(1)} %fusion.10) | copy-start | bytes 4718596
  91.2 5.6 %copy-start.13 = (bf16[1,384,2048]{2,1,0:T(8,128)(2,1)S(1)}, bf16[1,384,2048]{2,1,0:T(8,128)(2,1)}, u32[]{:S(2)}) copy-start(bf16[1,384,2048]{2,1,0:T(8,128)(2,1)} %param.12) | copy-start | bytes 4718596
  134.8 58.5 %all-to-all-start.2 = ((bf16[128,4,2048]{2,1,0:T(4,128)(2,1)}), bf16[128,4,2048]{2,1,0:T(4,128)(2,1)}, u32[]{:S(2)}, u32[]{:S(2)}) async-start(bf16[128,4,2048]{2,1,0:T(4,128)(2,1)} %reshape.71), calls=%async_computation.2 | async-start | bytes 4194304 | tf_op jit(solution)/shard_map/all_to_all | solution.py:15
  145.6 6.7 %copy-start.15 = (bf16[1,2048,384]{2,1,0:T(8,128)(2,1)S(1)}, bf16[1,2048,384]{2,1,0:T(8,128)(2,1)}, u32[]{:S(2)}) copy-start(bf16[1,2048,384]{2,1,0:T(8,128)(2,1)} %param.11) | copy-start | bytes 4718596
  152.4 4.2 %copy-start.6 = (bf16[512,768]{1,0:T(8,128)(2,1)}, bf16[512,768]{1,0:T(8,128)(2,1)S(1)}, u32[]{:S(2)}) copy-start(bf16[512,768]{1,0:T(8,128)(2,1)S(1)} %get-tuple-element.21) | copy-start | bytes 2359300
  152.4 4.2 %copy-start.9 = (bf16[512,768]{1,0:T(8,128)(2,1)}, bf16[512,768]{1,0:T(8,128)(2,1)S(1)}, u32[]{:S(2)}) copy-start(bf16[512,768]{1,0:T(8,128)(2,1)S(1)} %get-tuple-element.20) | copy-start | bytes 2359300
  152.4 4.2 %copy-start.16 = (bf16[1,2048,384]{2,1,0:T(8,128)(2,1)S(1)}, bf16[1,2048,384]{2,1,0:T(8,128)(2,1)}, u32[]{:S(2)}) copy-start(bf16[1,2048,384]{2,1,0:T(8,128)(2,1)} %param.10) | copy-start | bytes 4718596
  197.6 22.0 %collective-permute-start.5 = (f32[384,2048]{1,0:T(8,128)}, f32[384,2048]{1,0:T(8,128)}, u32[]{:S(2)}, u32[]{:S(2)}) collective-permute-start(f32[384,2048]{1,0:T(8,128)} %fusion.12), channel_id=1, source_target_pairs={{0,1},{1,0},{2,3},{3,2},{4,5},{5,4},{6,7},{7,6},{8,9},{9,8},{10,11... | collective-permute-start | bytes 9437192 | tf_op jit(solution)/shard_map/ppermute | solution.py:97
  197.6 59.7 %all-to-all-start.3 = ((bf16[128,4,2048]{2,1,0:T(4,128)(2,1)}), bf16[128,4,2048]{2,1,0:T(4,128)(2,1)}, u32[]{:S(2)}, u32[]{:S(2)}) async-start(bf16[128,4,2048]{2,1,0:T(4,128)(2,1)} %reshape.73), calls=%async_computation.3 | async-start | bytes 4194304 | tf_op jit(solution)/shard_map/all_to_all | solution.py:15
  204.6 4.2 %copy-start.7 = (bf16[512,768]{1,0:T(8,128)(2,1)S(1)}, bf16[512,768]{1,0:T(8,128)(2,1)}, u32[]{:S(2)}) copy-start(bf16[512,768]{1,0:T(8,128)(2,1)} %copy-done.6) | copy-start | bytes 2359300
  208.8 15.1 %collective-permute-start.3 = (f32[2048,384]{1,0:T(8,128)}, f32[2048,384]{1,0:T(8,128)}, u32[]{:S(2)}, u32[]{:S(2)}) collective-permute-start(f32[2048,384]{1,0:T(8,128)} %fusion.18), channel_id=1, source_target_pairs={{0,1},{1,0},{2,3},{3,2},{4,5},{5,4},{6,7},{7,6},{8,9},{9,8},{10,11... | collective-permute-start | bytes 9437192 | tf_op jit(solution)/shard_map/ppermute | solution.py:97
  211.7 16.5 %collective-permute-start.4 = (f32[2048,384]{1,0:T(8,128)}, f32[2048,384]{1,0:T(8,128)}, u32[]{:S(2)}, u32[]{:S(2)}) collective-permute-start(f32[2048,384]{1,0:T(8,128)} %fusion.15), channel_id=1, source_target_pairs={{0,1},{1,0},{2,3},{3,2},{4,5},{5,4},{6,7},{7,6},{8,9},{9,8},{10,11... | collective-permute-start | bytes 9437192 | tf_op jit(solution)/shard_map/ppermute | solution.py:97
  219.6 4.2 %copy-start.10 = (bf16[512,768]{1,0:T(8,128)(2,1)S(1)}, bf16[512,768]{1,0:T(8,128)(2,1)}, u32[]{:S(2)}) copy-start(bf16[512,768]{1,0:T(8,128)(2,1)} %copy-done.9) | copy-start | bytes 2359300
  223.8 4.4 %copy-start.8 = (bf16[512,768]{1,0:T(8,128)(2,1)S(1)}, bf16[512,768]{1,0:T(8,128)(2,1)}, u32[]{:S(2)}) copy-start(bf16[512,768]{1,0:T(8,128)(2,1)} %copy-done.6) | copy-start | bytes 2359300
  232.6 27.3 %copy-start.5 = (bf16[2,128,512]{2,1,0:T(8,128)(2,1)S(1)}, bf16[2,128,512]{2,1,0:T(8,128)(2,1)}, u32[]{:S(2)}) copy-start(bf16[2,128,512]{2,1,0:T(8,128)(2,1)} %copy-done.4) | copy-start | bytes 786436
  (4 other events, 11.5 us)

commit v4 on v3

--- a/solution.py
+++ b/solution.py
@@ -33,6 +33,11 @@
 
     wg_o, wu_o, wd_o = lax.ppermute((w_gate[0], w_up[0], w_down[0]), "core", swap)
     first = core == 0
+
+    def halves(value):
+        lo, hi = value[:, :half], value[:, half:]
+        return jnp.where(first, lo, hi), jnp.where(first, hi, lo)
+
     wg = jnp.where(first, jnp.concatenate([w_gate[0], wg_o], 1), jnp.concatenate([wg_o, w_gate[0]], 1))
     wu = jnp.where(first, jnp.concatenate([w_up[0], wu_o], 1), jnp.concatenate([wu_o, w_up[0]], 1))
     wd = jnp.where(first, jnp.concatenate([w_down[0], wd_o], 0), jnp.concatenate([wd_o, w_down[0]], 0))
@@ -78,21 +83,20 @@
         jnp.dot(dact, wg.T, preferred_element_type=f32)
         + jnp.dot(dupv, wu.T, preferred_element_type=f32)
     ).astype(jnp.bfloat16)
-    pgrad, o_back, dact, dupv, hidden = lax.optimization_barrier((pack(pgrad, chips), o_back, dact, dupv, hidden))
+    hid_m, hid_o = halves(hidden)
+    other_d = jnp.dot(hid_o.T, qrows, preferred_element_type=f32)
+    pgrad, o_back, dact, dupv, hid_m, other_d = lax.optimization_barrier(
+        (pack(pgrad, chips), o_back, dact, dupv, hid_m, other_d)
+    )
     o_back = unpack(o_back)
     p_back = unpack(to_chips(pgrad))
 
-    def halves(value):
-        lo, hi = value[:, :half], value[:, half:]
-        return jnp.where(first, lo, hi), jnp.where(first, hi, lo)
-
     dact_m, dact_o = halves(dact)
     dupv_m, dupv_o = halves(dupv)
-    hid_m, hid_o = halves(hidden)
     other = (
         jnp.dot(xrows.T, dact_o, preferred_element_type=f32),
         jnp.dot(xrows.T, dupv_o, preferred_element_type=f32),
-        jnp.dot(hid_o.T, qrows, preferred_element_type=f32),
+        other_d,
     )
     came = lax.ppermute(other, "core", swap)
     d_gate = (jnp.dot(xrows.T, dact_m, preferred_element_type=f32) + came[0]).astype(jnp.bfloat16)

time: 262 us -> 258 us (0.985)
  waiting for transfers between devices: 128 us -> 124 us
    all_to_all x4, waiting for transfers between devices: 128 us -> 124 us  [to_chips(): return lax.all_to_all(packed, CHIPS, 0, 0, tiled=True)]
  transfers between devices with their start and end apart: 10 -> 10, of which waited for: 5 -> 5; matrix products, arithmetic and copies ran while one was open for 31% -> 33% of each run, Pallas kernels for 0% -> 0%
where the time goes in v4:
time: 258 us; the launch traced here: 257 us
  waiting for transfers between devices  124 us (48%)
  matrix products  63.5 us (25%)
  starting transfers between devices  37 us (14%)
  local copies, waits for them, and re-layouts  29.9 us (12%)
    all_to_all x4, waiting for transfers between devices, to_chips(): return lax.all_to_all(packed, CHIPS, 0, 0, tiled=True)  124 us
    all_to_all x4, starting transfers between devices, to_chips(): return lax.all_to_all(packed, CHIPS, 0, 0, tiled=True)  35.8 us
    reshape x4, local copies, waits for them, and re-layouts, pack(): return rows.reshape(chips, -1, rows.shape[1])  14.6 us
    reshape x4, local copies, waits for them, and re-layouts, unpack(): return sent.reshape(-1, sent.shape[2])  13.1 us
    dot_general x1, matrix products, local(): dhid = jnp.dot(qrows, wd.T, preferred_element_type=f32)  6.7 us
    dot_general x1, matrix products, local(): upv = jnp.dot(xrows, wu, preferred_element_type=f32)  5.57 us
    dot_general x1, matrix products, local(): jnp.dot(dact, wg.T, preferred_element_type=f32)  5.24 us
    dot_general x1, matrix products, local(): outv = jnp.dot(hidden, wd, preferred_element_type=f32).astype(jnp.bfloat16)  5.16 us
  transfers between devices with their start and end apart: 10, of which 5 were waited for; matrix products, arithmetic and copies ran while one was open for 33% of the time, Pallas kernels for 0%

profile of v4, /device:TPU:32, one launch (start us, length us, event | category | flops | bytes accessed | tf_op | source)
XLA Modules:
  0.0 256.9 jit_solution(16012043839161683112)
XLA Ops:
  7.1 15.1 %all-to-all-start = ((bf16[128,4,2048]{2,1,0:T(4,128)(2,1)}), bf16[128,4,2048]{2,1,0:T(4,128)(2,1)S(1)}, u32[]{:S(2)}, u32[]{:S(2)}) async-start(bf16[128,4,2048]{2,1,0:T(4,128)(2,1)} %reshape.69), calls=%async_computation | async-start | bytes 4194304 | tf_op jit(solution)/shard_map/all_to_all | solution.py:15
  24.5 4.1 %reshape.68 = bf16[128,4,2048]{2,1,0:T(4,128)(2,1)} reshape(bf16[512,2048]{1,0:T(8,128)(2,1)} %bitcast_convert_fusion) | data formatting | bytes 4194304 | tf_op jit(solution)/shard_map/reshape | solution.py:11
  28.7 47.0 %all-to-all-done = bf16[128,4,2048]{2,1,0:T(4,128)(2,1)S(1)} async-done(((bf16[128,4,2048]{2,1,0:T(4,128)(2,1)}), bf16[128,4,2048]{2,1,0:T(4,128)(2,1)S(1)}, u32[]{:S(2)}, u32[]{:S(2)}) %all-to-all-start) | async-done | bytes 2097184 | tf_op jit(solution)/shard_map/all_to_all | solution.py:15
  75.7 6.9 %all-to-all-start.1 = ((bf16[128,4,2048]{2,1,0:T(4,128)(2,1)}), bf16[128,4,2048]{2,1,0:T(4,128)(2,1)}, u32[]{:S(2)}, u32[]{:S(2)}) async-start(bf16[128,4,2048]{2,1,0:T(4,128)(2,1)} %reshape.68), calls=%async_computation.1 | async-start | bytes 4194304 | tf_op jit(solution)/shard_map/all_to_all | solution.py:15
  86.4 4.8 %fusion.10 = f32[512,768]{1,0:T(8,128)S(1)} fusion(bf16[512,2048]{1,0:T(8,128)(2,1)S(1)} %reshape.70, bf16[2048,384]{1,0:T(8,128)(2,1)} %collective-permute-done, bf16[2048,384]{1,0:T(8,128)(2,1)} %bitcast.59, pred[]{:T(512)S(6)} %eq.62), kind=kOutput, calls=%fused_computation.27 | convolution fusion | flops 1624768512 | bytes 6815745 | tf_op jit(solution)/shard_map/dot_general | solution.py:69
  91.3 5.6 %multiply_convert_fusion.3 = (bf16[512,768]{1,0:T(8,128)(2,1)S(1)}, f32[512,768]{1,0:T(8,128)}) fusion(f32[512,768]{1,0:T(8,128)S(1)} %fusion.10, bf16[512,2048]{1,0:T(8,128)(2,1)S(1)} %reshape.70, bf16[2048,384]{1,0:T(8,128)(2,1)} %collective-permute-done.1, bf16[2048,384]{1,0:T(8,128)(2,1)S(1)} %bitcast.56, pred[]{:T(512)S(6)} %eq.62), kind=kOutput, calls=%fused_computation.18 | convolution fusion | flops 1627127808 | bytes 9175041 | tf_op jit(solution)/shard_map/dot_general | solution.py:70
  96.9 5.2 %convolution_convert_fusion.1 = bf16[512,2048]{1,0:T(8,128)(2,1)} fusion(bf16[512,768]{1,0:T(8,128)(2,1)S(1)} %get-tuple-element.29, bf16[384,2048]{1,0:T(8,128)(2,1)} %collective-permute-done.2, bf16[384,2048]{1,0:T(8,128)(2,1)S(1)} %bitcast.54, pred[]{:T(512)S(6)} %eq.62), kind=kOutput, calls=%fused_computation.9 | convolution fusion | flops 1625817088 | bytes 6029313 | tf_op jit(solution)/shard_map/dot_general | solution.py:74
  102.1 4.1 %reshape.71 = bf16[128,4,2048]{2,1,0:T(4,128)(2,1)} reshape(bf16[512,2048]{1,0:T(8,128)(2,1)} %convolution_convert_fusion.1) | data formatting | bytes 4194304 | tf_op jit(solution)/shard_map/reshape | solution.py:11
  106.1 28.7 %all-to-all-done.1 = bf16[128,4,2048]{2,1,0:T(4,128)(2,1)} async-done(((bf16[128,4,2048]{2,1,0:T(4,128)(2,1)}), bf16[128,4,2048]{2,1,0:T(4,128)(2,1)}, u32[]{:S(2)}, u32[]{:S(2)}) %all-to-all-start.1) | async-done | bytes 2097184 | tf_op jit(solution)/shard_map/all_to_all | solution.py:15
  134.8 6.9 %all-to-all-start.2 = ((bf16[128,4,2048]{2,1,0:T(4,128)(2,1)}), bf16[128,4,2048]{2,1,0:T(4,128)(2,1)}, u32[]{:S(2)}, u32[]{:S(2)}) async-start(bf16[128,4,2048]{2,1,0:T(4,128)(2,1)} %reshape.71), calls=%async_computation.2 | async-start | bytes 4194304 | tf_op jit(solution)/shard_map/all_to_all | solution.py:15
  141.7 3.9 %reshape.72 = bf16[512,2048]{1,0:T(8,128)(2,1)} reshape(bf16[128,4,2048]{2,1,0:T(4,128)(2,1)} %all-to-all-done.1) | data formatting | bytes 4194304 | tf_op jit(solution)/shard_map/reshape | solution.py:19
  145.7 6.7 %multiply_convert_fusion.2 = (bf16[512,768]{1,0:T(8,128)(2,1)S(1)}, bf16[512,768]{1,0:T(8,128)(2,1)S(1)}) fusion(f32[512,768]{1,0:T(8,128)} %copy-done.16, f32[512,768]{1,0:T(8,128)} %get-tuple-element.30, bf16[512,2048]{1,0:T(8,128)(2,1)} %reshape.72, bf16[384,2048]{1,0:T(8,128)(2,1)} %collective-permute-done.2, bf16[384,2048]{1,0:T(8,128)(2,1)} %bitcast.53, ...), kind=kOutput, calls=%fused_computation.17 | convolution fusion | flops 1629880320 | bytes 9961473 | tf_op jit(solution)/shard_map/dot_general | solution.py:79
  152.5 4.2 %fusion.8 = f32[512,2048]{1,0:T(8,128)S(1)} fusion(bf16[512,768]{1,0:T(8,128)(2,1)S(1)} %get-tuple-element.22, bf16[2048,384]{1,0:T(8,128)(2,1)} %collective-permute-done.1, bf16[2048,384]{1,0:T(8,128)(2,1)S(1)} %bitcast.57, pred[]{:T(512)S(6)} %eq.62), kind=kOutput, calls=%fused_computation.25 | convolution fusion | flops 1624768512 | bytes 8126465 | tf_op jit(solution)/shard_map/dot_general | solution.py:84
  156.6 5.2 %add_convert_fusion = bf16[512,2048]{1,0:T(8,128)(2,1)} fusion(f32[512,2048]{1,0:T(8,128)S(1)} %fusion.8, bf16[512,768]{1,0:T(8,128)(2,1)S(1)} %get-tuple-element.21, bf16[2048,384]{1,0:T(8,128)(2,1)} %collective-permute-done, bf16[2048,384]{1,0:T(8,128)(2,1)S(1)} %bitcast.60, pred[]{:T(512)S(6)} %eq.62), kind=kOutput, calls=%fused_computation.1 | convolution fusion | flops 1626865664 | bytes 10223617 | tf_op jit(solution)/shard_map/dot_general | solution.py:83
  161.9 4.1 %reshape.73 = bf16[128,4,2048]{2,1,0:T(4,128)(2,1)} reshape(bf16[512,2048]{1,0:T(8,128)(2,1)} %add_convert_fusion) | data formatting | bytes 4194304 | tf_op jit(solution)/shard_map/reshape | solution.py:11
  166.0 4.2 %fusion.18 = f32[384,2048]{1,0:T(8,128)} fusion(bf16[512,2048]{1,0:T(8,128)(2,1)} %reshape.72, pred[]{:T(512)S(6)} %eq.62, bf16[512,768]{1,0:T(8,128)(2,1)S(1)} %get-tuple-element.29), kind=kOutput, calls=%fused_computation.37 | convolution fusion | flops 805502976 | bytes 6029313 | tf_op jit(solution)/shard_map/dot_general | solution.py:87
  170.3 23.1 %all-to-all-done.2 = bf16[128,4,2048]{2,1,0:T(4,128)(2,1)} async-done(((bf16[128,4,2048]{2,1,0:T(4,128)(2,1)}), bf16[128,4,2048]{2,1,0:T(4,128)(2,1)}, u32[]{:S(2)}, u32[]{:S(2)}) %all-to-all-start.2) | async-done | bytes 2097184 | tf_op jit(solution)/shard_map/all_to_all | solution.py:15
  193.4 6.9 %all-to-all-start.3 = ((bf16[128,4,2048]{2,1,0:T(4,128)(2,1)}), bf16[128,4,2048]{2,1,0:T(4,128)(2,1)}, u32[]{:S(2)}, u32[]{:S(2)}) async-start(bf16[128,4,2048]{2,1,0:T(4,128)(2,1)} %reshape.73), calls=%async_computation.3 | async-start | bytes 4194304 | tf_op jit(solution)/shard_map/all_to_all | solution.py:15
  200.3 4.2 %fusion.15 = f32[2048,384]{1,0:T(8,128)} fusion(bf16[512,2048]{1,0:T(8,128)(2,1)S(1)} %reshape.70, pred[]{:T(512)S(6)} %eq.62, bf16[512,768]{1,0:T(8,128)(2,1)} %copy-done.8), kind=kOutput, calls=%fused_computation.34 | convolution fusion | flops 805502976 | bytes 6029313 | tf_op jit(solution)/shard_map/dot_general | solution.py:97
  207.9 4.0 %reshape.77 = bf16[512,2048,1]{1,0,2:T(8,128)(2,1)} reshape(bf16[128,4,2048]{2,1,0:T(4,128)(2,1)} %all-to-all-done.2) | data formatting | bytes 4194304 | tf_op jit(solution)/shard_map/reshape | solution.py:19
  215.4 4.1 %fusion.2 = bf16[1,384,2048]{2,1,0:T(8,128)(2,1)} fusion(f32[384,2048]{1,0:T(8,128)} %collective-permute-done.5, bf16[512,384]{1,0:T(8,128)(2,1)S(1)} %broadcast_select_fusion, bf16[512,2048]{1,0:T(8,128)(2,1)S(1)} %copy-done.2), kind=kOutput, calls=%fused_computation.13 | convolution fusion | flops 806879232 | bytes 7208960 | tf_op jit(solution)/shard_map/dot_general | solution.py:104
  219.5 4.3 %fusion = bf16[1,2048,384]{2,1,0:T(8,128)(2,1)} fusion(f32[2048,384]{1,0:T(8,128)} %collective-permute-done.3, bf16[512,2048]{1,0:T(8,128)(2,1)S(1)} %reshape.70, pred[]{:T(512)S(6)} %eq.62, bf16[512,768]{1,0:T(8,128)(2,1)S(1)} %copy-done.9), kind=kOutput, calls=%fused_computation.11 | convolution fusion | flops 807075840 | bytes 7602177 | tf_op jit(solution)/shard_map/dot_general | solution.py:102
  223.9 4.3 %fusion.1 = bf16[1,2048,384]{2,1,0:T(8,128)(2,1)} fusion(f32[2048,384]{1,0:T(8,128)} %collective-permute-done.4, bf16[512,2048]{1,0:T(8,128)(2,1)S(1)} %reshape.70, pred[]{:T(512)S(6)} %eq.62, bf16[512,768]{1,0:T(8,128)(2,1)S(1)} %copy-done.7), kind=kOutput, calls=%fused_computation.12 | convolution fusion | flops 807075840 | bytes 7602177 | tf_op jit(solution)/shard_map/dot_general | solution.py:103
  228.2 24.8 %all-to-all-done.3 = bf16[128,4,2048]{2,1,0:T(4,128)(2,1)} async-done(((bf16[128,4,2048]{2,1,0:T(4,128)(2,1)}), bf16[128,4,2048]{2,1,0:T(4,128)(2,1)}, u32[]{:S(2)}, u32[]{:S(2)}) %all-to-all-start.3) | async-done | bytes 2097184 | tf_op jit(solution)/shard_map/all_to_all | solution.py:15
  (73 shorter events, 23.3 us)
Async XLA Ops:
  7.1 15.2 %copy-start.10 = (bf16[128,2048]{1,0:T(8,128)(2,1)S(1)}, bf16[128,2048]{1,0:T(8,128)(2,1)}, u32[]{:S(2)}) copy-start(bf16[128,2048]{1,0:T(8,128)(2,1)} %param.13) | copy-start | bytes 1572868
  7.1 15.3 %copy-start.11 = (s32[128,2]{0,1:T(2,128)S(1)}, s32[128,2]{0,1:T(2,128)}, u32[]{:S(2)}) copy-start(s32[128,2]{0,1:T(2,128)} %param.9) | copy-start | bytes 3076
  7.1 68.6 %all-to-all-start = ((bf16[128,4,2048]{2,1,0:T(4,128)(2,1)}), bf16[128,4,2048]{2,1,0:T(4,128)(2,1)S(1)}, u32[]{:S(2)}, u32[]{:S(2)}) async-start(bf16[128,4,2048]{2,1,0:T(4,128)(2,1)} %reshape.69), calls=%async_computation | async-start | bytes 4194304 | tf_op jit(solution)/shard_map/all_to_all | solution.py:15
  75.7 6.9 %copy-start.3 = (bf16[128,4,2048]{2,1,0:T(4,128)(2,1)}, bf16[128,4,2048]{2,1,0:T(4,128)(2,1)S(1)}, u32[]{:S(2)}) copy-start(bf16[128,4,2048]{2,1,0:T(4,128)(2,1)S(1)} %all-to-all-done) | copy-start | bytes 6291460
  75.7 59.1 %all-to-all-start.1 = ((bf16[128,4,2048]{2,1,0:T(4,128)(2,1)}), bf16[128,4,2048]{2,1,0:T(4,128)(2,1)}, u32[]{:S(2)}, u32[]{:S(2)}) async-start(bf16[128,4,2048]{2,1,0:T(4,128)(2,1)} %reshape.68), calls=%async_computation.1 | async-start | bytes 4194304 | tf_op jit(solution)/shard_map/all_to_all | solution.py:15
  82.6 3.8 %collective-permute-start = (bf16[2048,384]{1,0:T(8,128)(2,1)}, bf16[2048,384]{1,0:T(8,128)(2,1)}, u32[]{:S(2)}, u32[]{:S(2)}) collective-permute-start(bf16[2048,384]{1,0:T(8,128)(2,1)} %bitcast.58), channel_id=1, source_target_pairs={{0,1},{1,0},{2,3},{3,2},{4,5},{5,4},{6,7},{7,6},{8,9},{9,8},{10,11... | collective-permute-start | bytes 4718600 | tf_op jit(solution)/shard_map/ppermute | solution.py:34
  82.7 8.6 %collective-permute-start.1 = (bf16[2048,384]{1,0:T(8,128)(2,1)}, bf16[2048,384]{1,0:T(8,128)(2,1)}, u32[]{:S(2)}, u32[]{:S(2)}) collective-permute-start(bf16[2048,384]{1,0:T(8,128)(2,1)} %bitcast.55), channel_id=1, source_target_pairs={{0,1},{1,0},{2,3},{3,2},{4,5},{5,4},{6,7},{7,6},{8,9},{9,8},{10,11... | collective-permute-start | bytes 4718600 | tf_op jit(solution)/shard_map/ppermute | solution.py:34
  83.2 13.7 %collective-permute-start.2 = (bf16[384,2048]{1,0:T(8,128)(2,1)}, bf16[384,2048]{1,0:T(8,128)(2,1)}, u32[]{:S(2)}, u32[]{:S(2)}) collective-permute-start(bf16[384,2048]{1,0:T(8,128)(2,1)} %bitcast.52), channel_id=1, source_target_pairs={{0,1},{1,0},{2,3},{3,2},{4,5},{5,4},{6,7},{7,6},{8,9},{9,8},{10,11... | collective-permute-start | bytes 4718600 | tf_op jit(solution)/shard_map/ppermute | solution.py:34
  85.8 5.5 %copy-start.13 = (bf16[1,2048,384]{2,1,0:T(8,128)(2,1)S(1)}, bf16[1,2048,384]{2,1,0:T(8,128)(2,1)}, u32[]{:S(2)}) copy-start(bf16[1,2048,384]{2,1,0:T(8,128)(2,1)} %param.11) | copy-start | bytes 4718596
  91.3 5.6 %copy-start.16 = (f32[512,768]{1,0:T(8,128)}, f32[512,768]{1,0:T(8,128)S(1)}, u32[]{:S(2)}) copy-start(f32[512,768]{1,0:T(8,128)S(1)} %fusion.10) | copy-start | bytes 4718596
  91.3 5.6 %copy-start.12 = (bf16[1,384,2048]{2,1,0:T(8,128)(2,1)S(1)}, bf16[1,384,2048]{2,1,0:T(8,128)(2,1)}, u32[]{:S(2)}) copy-start(bf16[1,384,2048]{2,1,0:T(8,128)(2,1)} %param.12) | copy-start | bytes 4718596
  134.8 58.5 %all-to-all-start.2 = ((bf16[128,4,2048]{2,1,0:T(4,128)(2,1)}), bf16[128,4,2048]{2,1,0:T(4,128)(2,1)}, u32[]{:S(2)}, u32[]{:S(2)}) async-start(bf16[128,4,2048]{2,1,0:T(4,128)(2,1)} %reshape.71), calls=%async_computation.2 | async-start | bytes 4194304 | tf_op jit(solution)/shard_map/all_to_all | solution.py:15
  145.7 6.7 %copy-start.14 = (bf16[1,2048,384]{2,1,0:T(8,128)(2,1)S(1)}, bf16[1,2048,384]{2,1,0:T(8,128)(2,1)}, u32[]{:S(2)}) copy-start(bf16[1,2048,384]{2,1,0:T(8,128)(2,1)} %param.11) | copy-start | bytes 4718596
  152.4 4.2 %copy-start.6 = (bf16[512,768]{1,0:T(8,128)(2,1)}, bf16[512,768]{1,0:T(8,128)(2,1)S(1)}, u32[]{:S(2)}) copy-start(bf16[512,768]{1,0:T(8,128)(2,1)S(1)} %get-tuple-element.22) | copy-start | bytes 2359300
  152.4 4.2 %copy-start.8 = (bf16[512,768]{1,0:T(8,128)(2,1)}, bf16[512,768]{1,0:T(8,128)(2,1)S(1)}, u32[]{:S(2)}) copy-start(bf16[512,768]{1,0:T(8,128)(2,1)S(1)} %get-tuple-element.21) | copy-start | bytes 2359300
  152.4 4.2 %copy-start.15 = (bf16[1,2048,384]{2,1,0:T(8,128)(2,1)S(1)}, bf16[1,2048,384]{2,1,0:T(8,128)(2,1)}, u32[]{:S(2)}) copy-start(bf16[1,2048,384]{2,1,0:T(8,128)(2,1)} %param.10) | copy-start | bytes 4718596
  193.4 22.0 %collective-permute-start.5 = (f32[384,2048]{1,0:T(8,128)}, f32[384,2048]{1,0:T(8,128)}, u32[]{:S(2)}, u32[]{:S(2)}) collective-permute-start(f32[384,2048]{1,0:T(8,128)} %fusion.18), channel_id=1, source_target_pairs={{0,1},{1,0},{2,3},{3,2},{4,5},{5,4},{6,7},{7,6},{8,9},{9,8},{10,11... | collective-permute-start | bytes 9437192 | tf_op jit(solution)/shard_map/ppermute | solution.py:101
  193.4 59.7 %all-to-all-start.3 = ((bf16[128,4,2048]{2,1,0:T(4,128)(2,1)}), bf16[128,4,2048]{2,1,0:T(4,128)(2,1)}, u32[]{:S(2)}, u32[]{:S(2)}) async-start(bf16[128,4,2048]{2,1,0:T(4,128)(2,1)} %reshape.73), calls=%async_computation.3 | async-start | bytes 4194304 | tf_op jit(solution)/shard_map/all_to_all | solution.py:15
  200.3 4.3 %copy-start.7 = (bf16[512,768]{1,0:T(8,128)(2,1)S(1)}, bf16[512,768]{1,0:T(8,128)(2,1)}, u32[]{:S(2)}) copy-start(bf16[512,768]{1,0:T(8,128)(2,1)} %copy-done.6) | copy-start | bytes 2359300
  204.5 15.0 %collective-permute-start.3 = (f32[2048,384]{1,0:T(8,128)}, f32[2048,384]{1,0:T(8,128)}, u32[]{:S(2)}, u32[]{:S(2)}) collective-permute-start(f32[2048,384]{1,0:T(8,128)} %fusion.15), channel_id=1, source_target_pairs={{0,1},{1,0},{2,3},{3,2},{4,5},{5,4},{6,7},{7,6},{8,9},{9,8},{10,11... | collective-permute-start | bytes 9437192 | tf_op jit(solution)/shard_map/ppermute | solution.py:101
  207.5 16.4 %collective-permute-start.4 = (f32[2048,384]{1,0:T(8,128)}, f32[2048,384]{1,0:T(8,128)}, u32[]{:S(2)}, u32[]{:S(2)}) collective-permute-start(f32[2048,384]{1,0:T(8,128)} %fusion.12), channel_id=1, source_target_pairs={{0,1},{1,0},{2,3},{3,2},{4,5},{5,4},{6,7},{7,6},{8,9},{9,8},{10,11... | collective-permute-start | bytes 9437192 | tf_op jit(solution)/shard_map/ppermute | solution.py:101
  215.4 4.2 %copy-start.9 = (bf16[512,768]{1,0:T(8,128)(2,1)S(1)}, bf16[512,768]{1,0:T(8,128)(2,1)}, u32[]{:S(2)}) copy-start(bf16[512,768]{1,0:T(8,128)(2,1)} %copy-done.8) | copy-start | bytes 2359300
  228.2 27.4 %copy-start.5 = (bf16[2,128,512]{2,1,0:T(8,128)(2,1)S(1)}, bf16[2,128,512]{2,1,0:T(8,128)(2,1)}, u32[]{:S(2)}) copy-start(bf16[2,128,512]{2,1,0:T(8,128)(2,1)} %copy-done.4) | copy-start | bytes 786436
  253.0 3.9 %copy-start.1 = (bf16[128,2048]{1,0:T(8,128)(2,1)S(1)}, bf16[128,2048]{1,0:T(8,128)(2,1)}, u32[]{:S(2)}) copy-start(bf16[128,2048]{1,0:T(8,128)(2,1)} %param.7) | copy-start | bytes 1572868
  (3 other events, 7.7 us)

commit v5 on v2

--- a/solution.py
+++ b/solution.py
@@ -38,9 +38,9 @@
     wd = jnp.where(first, jnp.concatenate([w_down[0], wd_o], 0), jnp.concatenate([wd_o, w_down[0]], 0))
 
     expert_ids = routes.reshape(pairs)
-    onehot = (expert_ids[:, None] == jnp.arange(chips, dtype=jnp.int32)[None, :]).astype(jnp.int32)
-    before = jnp.cumsum(onehot, axis=0) - onehot
-    position = jnp.sum(before * onehot, axis=1)
+    order = jnp.arange(pairs, dtype=jnp.int32)
+    earlier = (expert_ids[:, None] == expert_ids[None, :]) & (order[None, :] < order[:, None])
+    position = jnp.sum(earlier.astype(jnp.int32), axis=1)
     slot = expert_ids * most + position
     gates = gate_codes.reshape(pairs).astype(f32) / 1024.0
     qpairs = (

time: 256 us -> 255 us (level)
    unnamed x46 -> x45, local copies, waits for them, and re-layouts: 5.94 us -> 5.97 us
where the time goes in v5:
time: 255 us; the launch traced here: 254 us
  waiting for transfers between devices  118 us (46%)
  matrix products  44.7 us (18%)
  starting transfers between devices  37 us (15%)
  local copies, waits for them, and re-layouts  32.4 us (13%)
  other arithmetic  21 us (8%)
    all_to_all x4, waiting for transfers between devices, to_chips(): return lax.all_to_all(packed, CHIPS, 0, 0, tiled=True)  117 us
    all_to_all x4, starting transfers between devices, to_chips(): return lax.all_to_all(packed, CHIPS, 0, 0, tiled=True)  35.8 us
    reshape x4, local copies, waits for them, and re-layouts, pack(): return rows.reshape(chips, -1, rows.shape[1])  14.6 us
    broadcast_in_dim x3, other arithmetic, local(): return (mixed, d_tokens, d_gate[None], d_up[None], d_down[None])  13.4 us
    reshape x4, local copies, waits for them, and re-layouts, unpack(): return sent.reshape(-1, sent.shape[2])  11.5 us
    dot_general x1, matrix products, local(): dhid = jnp.dot(qrows, wd.T, preferred_element_type=f32)  6.71 us
    unnamed x45, local copies, waits for them, and re-layouts  5.97 us
    dot_general x1, matrix products, local(): upv = jnp.dot(xrows, wu, preferred_element_type=f32)  5.57 us
  transfers between devices with their start and end apart: 10, of which 5 were waited for; matrix products, arithmetic and copies ran while one was open for 33% of the time, Pallas kernels for 0%

profile of v5, /device:TPU:32, one launch (start us, length us, event | category | flops | bytes accessed | tf_op | source)
XLA Modules:
  0.0 254.1 jit_solution(8423441999499528234)
XLA Ops:
  5.8 15.1 %all-to-all-start = ((bf16[128,4,2048]{2,1,0:T(4,128)(2,1)}), bf16[128,4,2048]{2,1,0:T(4,128)(2,1)S(1)}, u32[]{:S(2)}, u32[]{:S(2)}) async-start(bf16[128,4,2048]{2,1,0:T(4,128)(2,1)} %reshape.53), calls=%async_computation | async-start | bytes 4194304 | tf_op jit(solution)/shard_map/all_to_all | solution.py:15
  23.3 4.1 %reshape.52 = bf16[128,4,2048]{2,1,0:T(4,128)(2,1)} reshape(bf16[512,2048]{1,0:T(8,128)(2,1)} %bitcast_convert_fusion) | data formatting | bytes 4194304 | tf_op jit(solution)/shard_map/reshape | solution.py:11
  27.4 47.0 %all-to-all-done = bf16[128,4,2048]{2,1,0:T(4,128)(2,1)S(1)} async-done(((bf16[128,4,2048]{2,1,0:T(4,128)(2,1)}), bf16[128,4,2048]{2,1,0:T(4,128)(2,1)S(1)}, u32[]{:S(2)}, u32[]{:S(2)}) %all-to-all-start) | async-done | bytes 2097184 | tf_op jit(solution)/shard_map/all_to_all | solution.py:15
  74.4 6.9 %all-to-all-start.1 = ((bf16[128,4,2048]{2,1,0:T(4,128)(2,1)}), bf16[128,4,2048]{2,1,0:T(4,128)(2,1)}, u32[]{:S(2)}, u32[]{:S(2)}) async-start(bf16[128,4,2048]{2,1,0:T(4,128)(2,1)} %reshape.52), calls=%async_computation.1 | async-start | bytes 4194304 | tf_op jit(solution)/shard_map/all_to_all | solution.py:15
  82.0 2.5 reshape.54
  85.1 4.8 %fusion.10 = f32[512,768]{1,0:T(8,128)S(1)} fusion(bf16[512,2048]{1,0:T(8,128)(2,1)S(1)} %reshape.54, bf16[2048,384]{1,0:T(8,128)(2,1)} %collective-permute-done, bf16[2048,384]{1,0:T(8,128)(2,1)} %bitcast.46, pred[]{:T(512)S(6)} %eq.48), kind=kOutput, calls=%fused_computation.30 | convolution fusion | flops 1624768512 | bytes 6815745 | tf_op jit(solution)/shard_map/dot_general | solution.py:64
  90.0 5.6 %multiply_convert_fusion.3 = (bf16[512,768]{1,0:T(8,128)(2,1)S(1)}, f32[512,768]{1,0:T(8,128)}) fusion(f32[512,768]{1,0:T(8,128)S(1)} %fusion.10, bf16[512,2048]{1,0:T(8,128)(2,1)S(1)} %reshape.54, bf16[2048,384]{1,0:T(8,128)(2,1)} %collective-permute-done.1, bf16[2048,384]{1,0:T(8,128)(2,1)S(1)} %bitcast.43, pred[]{:T(512)S(6)} %eq.48), kind=kOutput, calls=%fused_computation.21 | convolution fusion | flops 1627127808 | bytes 9175041 | tf_op jit(solution)/shard_map/dot_general | solution.py:65
  96.4 5.2 %convolution_convert_fusion.1 = bf16[512,2048]{1,0:T(8,128)(2,1)} fusion(bf16[512,768]{1,0:T(8,128)(2,1)S(1)} %get-tuple-element.22, bf16[384,2048]{1,0:T(8,128)(2,1)} %collective-permute-done.2, bf16[384,2048]{1,0:T(8,128)(2,1)S(1)} %bitcast.41, pred[]{:T(512)S(6)} %eq.48), kind=kOutput, calls=%fused_computation.9 | convolution fusion | flops 1625817088 | bytes 6029313 | tf_op jit(solution)/shard_map/dot_general | solution.py:69
  101.6 4.1 %reshape.55 = bf16[128,4,2048]{2,1,0:T(4,128)(2,1)} reshape(bf16[512,2048]{1,0:T(8,128)(2,1)} %convolution_convert_fusion.1) | data formatting | bytes 4194304 | tf_op jit(solution)/shard_map/reshape | solution.py:11
  105.8 27.8 %all-to-all-done.1 = bf16[128,4,2048]{2,1,0:T(4,128)(2,1)} async-done(((bf16[128,4,2048]{2,1,0:T(4,128)(2,1)}), bf16[128,4,2048]{2,1,0:T(4,128)(2,1)}, u32[]{:S(2)}, u32[]{:S(2)}) %all-to-all-start.1) | async-done | bytes 2097184 | tf_op jit(solution)/shard_map/all_to_all | solution.py:15
  133.6 6.9 %all-to-all-start.2 = ((bf16[128,4,2048]{2,1,0:T(4,128)(2,1)}), bf16[128,4,2048]{2,1,0:T(4,128)(2,1)}, u32[]{:S(2)}, u32[]{:S(2)}) async-start(bf16[128,4,2048]{2,1,0:T(4,128)(2,1)} %reshape.55), calls=%async_computation.2 | async-start | bytes 4194304 | tf_op jit(solution)/shard_map/all_to_all | solution.py:15
  140.4 3.9 %reshape.56 = bf16[512,2048]{1,0:T(8,128)(2,1)} reshape(bf16[128,4,2048]{2,1,0:T(4,128)(2,1)} %all-to-all-done.1) | data formatting | bytes 4194304 | tf_op jit(solution)/shard_map/reshape | solution.py:19
  144.4 6.7 %multiply_convert_fusion.2 = (bf16[512,768]{1,0:T(8,128)(2,1)S(1)}, bf16[512,768]{1,0:T(8,128)(2,1)S(1)}) fusion(f32[512,768]{1,0:T(8,128)} %copy-done.17, f32[512,768]{1,0:T(8,128)} %get-tuple-element.28, bf16[512,2048]{1,0:T(8,128)(2,1)} %reshape.56, bf16[384,2048]{1,0:T(8,128)(2,1)} %collective-permute-done.2, bf16[384,2048]{1,0:T(8,128)(2,1)} %bitcast.40, ...), kind=kOutput, calls=%fused_computation.20 | convolution fusion | flops 1629880320 | bytes 9961473 | tf_op jit(solution)/shard_map/dot_general | solution.py:74
  151.2 4.2 %fusion.8 = f32[512,2048]{1,0:T(8,128)S(1)} fusion(bf16[512,768]{1,0:T(8,128)(2,1)S(1)} %get-tuple-element.21, bf16[2048,384]{1,0:T(8,128)(2,1)} %collective-permute-done.1, bf16[2048,384]{1,0:T(8,128)(2,1)S(1)} %bitcast.44, pred[]{:T(512)S(6)} %eq.48), kind=kOutput, calls=%fused_computation.28 | convolution fusion | flops 1624768512 | bytes 8126465 | tf_op jit(solution)/shard_map/dot_general | solution.py:79
  155.3 5.2 %add_convert_fusion = bf16[512,2048]{1,0:T(8,128)(2,1)} fusion(f32[512,2048]{1,0:T(8,128)S(1)} %fusion.8, bf16[512,768]{1,0:T(8,128)(2,1)S(1)} %get-tuple-element.20, bf16[2048,384]{1,0:T(8,128)(2,1)} %collective-permute-done, bf16[2048,384]{1,0:T(8,128)(2,1)S(1)} %bitcast.47, pred[]{:T(512)S(6)} %eq.48), kind=kOutput, calls=%fused_computation.1 | convolution fusion | flops 1626865664 | bytes 10223617 | tf_op jit(solution)/shard_map/dot_general | solution.py:78
  160.5 4.1 %reshape.57 = bf16[128,4,2048]{2,1,0:T(4,128)(2,1)} reshape(bf16[512,2048]{1,0:T(8,128)(2,1)} %add_convert_fusion) | data formatting | bytes 4194304 | tf_op jit(solution)/shard_map/reshape | solution.py:11
  164.6 27.5 %all-to-all-done.2 = bf16[128,4,2048]{2,1,0:T(4,128)(2,1)} async-done(((bf16[128,4,2048]{2,1,0:T(4,128)(2,1)}), bf16[128,4,2048]{2,1,0:T(4,128)(2,1)}, u32[]{:S(2)}, u32[]{:S(2)}) %all-to-all-start.2) | async-done | bytes 2097184 | tf_op jit(solution)/shard_map/all_to_all | solution.py:15
  192.1 6.9 %all-to-all-start.3 = ((bf16[128,4,2048]{2,1,0:T(4,128)(2,1)}), bf16[128,4,2048]{2,1,0:T(4,128)(2,1)}, u32[]{:S(2)}, u32[]{:S(2)}) async-start(bf16[128,4,2048]{2,1,0:T(4,128)(2,1)} %reshape.57), calls=%async_computation.3 | async-start | bytes 4194304 | tf_op jit(solution)/shard_map/all_to_all | solution.py:15
  199.1 3.7 %fusion.27 = f32[768,2048]{1,0:T(8,128)S(1)} fusion(bf16[512,768]{1,0:T(8,128)(2,1)} %copy-done.6, bf16[512,2048]{1,0:T(8,128)(2,1)} %reshape.56), kind=kOutput, calls=%fused_computation.52 | convolution fusion | flops 1610612736 | bytes 9175040 | tf_op jit(solution)/shard_map/dot_general | solution.py:87
  221.8 5.8 %fusion.2 = bf16[1,384,2048]{2,1,0:T(8,128)(2,1)} fusion(f32[384,2048]{1,0:T(8,128)} %collective-permute-done.5, f32[768,2048]{1,0:T(8,128)} %copy-done.4, pred[]{:T(512)S(6)} %eq.48), kind=kLoop, calls=%fused_computation.18 | loop fusion | flops 2359296 | bytes 11010049 | tf_op jit(solution)/shard_map/broadcast_in_dim | solution.py:101
  227.6 3.9 %fusion = bf16[1,2048,384]{2,1,0:T(8,128)(2,1)} fusion(f32[2048,384]{1,0:T(8,128)} %collective-permute-done.3, f32[2048,768]{1,0:T(8,128)S(1)} %bitcast.36, pred[]{:T(512)S(6)} %eq.48), kind=kLoop, calls=%fused_computation.16 | loop fusion | flops 2359296 | bytes 11010049 | tf_op jit(solution)/shard_map/broadcast_in_dim | solution.py:101
  231.5 3.8 %fusion.1 = bf16[1,2048,384]{2,1,0:T(8,128)(2,1)} fusion(f32[2048,384]{1,0:T(8,128)} %collective-permute-done.4, f32[2048,768]{1,0:T(8,128)S(1)} %bitcast.34, pred[]{:T(512)S(6)} %eq.48), kind=kLoop, calls=%fused_computation.17 | loop fusion | flops 2359296 | bytes 11010049 | tf_op jit(solution)/shard_map/broadcast_in_dim | solution.py:101
  235.3 15.1 %all-to-all-done.3 = bf16[128,4,2048]{2,1,0:T(4,128)(2,1)} async-done(((bf16[128,4,2048]{2,1,0:T(4,128)(2,1)}), bf16[128,4,2048]{2,1,0:T(4,128)(2,1)}, u32[]{:S(2)}, u32[]{:S(2)}) %all-to-all-start.3) | async-done | bytes 2097184 | tf_op jit(solution)/shard_map/all_to_all | solution.py:15
  250.4 2.5 reshape.59
  (78 shorter events, 29.9 us)
Async XLA Ops:
  3.6 17.4 %copy-start.11 = (bf16[128,2048]{1,0:T(8,128)(2,1)S(1)}, bf16[128,2048]{1,0:T(8,128)(2,1)}, u32[]{:S(2)}) copy-start(bf16[128,2048]{1,0:T(8,128)(2,1)} %param.13) | copy-start | bytes 1572868
  5.8 15.3 %copy-start.12 = (s32[128,2]{0,1:T(2,128)S(1)}, s32[128,2]{0,1:T(2,128)}, u32[]{:S(2)}) copy-start(s32[128,2]{0,1:T(2,128)} %param.9) | copy-start | bytes 3076
  5.8 68.6 %all-to-all-start = ((bf16[128,4,2048]{2,1,0:T(4,128)(2,1)}), bf16[128,4,2048]{2,1,0:T(4,128)(2,1)S(1)}, u32[]{:S(2)}, u32[]{:S(2)}) async-start(bf16[128,4,2048]{2,1,0:T(4,128)(2,1)} %reshape.53), calls=%async_computation | async-start | bytes 4194304 | tf_op jit(solution)/shard_map/all_to_all | solution.py:15
  74.4 7.6 %copy-start.5 = (bf16[128,4,2048]{2,1,0:T(4,128)(2,1)}, bf16[128,4,2048]{2,1,0:T(4,128)(2,1)S(1)}, u32[]{:S(2)}) copy-start(bf16[128,4,2048]{2,1,0:T(4,128)(2,1)S(1)} %all-to-all-done) | copy-start | bytes 6291460
  74.4 59.1 %all-to-all-start.1 = ((bf16[128,4,2048]{2,1,0:T(4,128)(2,1)}), bf16[128,4,2048]{2,1,0:T(4,128)(2,1)}, u32[]{:S(2)}, u32[]{:S(2)}) async-start(bf16[128,4,2048]{2,1,0:T(4,128)(2,1)} %reshape.52), calls=%async_computation.1 | async-start | bytes 4194304 | tf_op jit(solution)/shard_map/all_to_all | solution.py:15
  81.3 3.8 %collective-permute-start = (bf16[2048,384]{1,0:T(8,128)(2,1)}, bf16[2048,384]{1,0:T(8,128)(2,1)}, u32[]{:S(2)}, u32[]{:S(2)}) collective-permute-start(bf16[2048,384]{1,0:T(8,128)(2,1)} %bitcast.45), channel_id=1, source_target_pairs={{0,1},{1,0},{2,3},{3,2},{4,5},{5,4},{6,7},{7,6},{8,9},{9,8},{10,11... | collective-permute-start | bytes 4718600 | tf_op jit(solution)/shard_map/ppermute | solution.py:34
  81.4 8.5 %collective-permute-start.1 = (bf16[2048,384]{1,0:T(8,128)(2,1)}, bf16[2048,384]{1,0:T(8,128)(2,1)}, u32[]{:S(2)}, u32[]{:S(2)}) collective-permute-start(bf16[2048,384]{1,0:T(8,128)(2,1)} %bitcast.42), channel_id=1, source_target_pairs={{0,1},{1,0},{2,3},{3,2},{4,5},{5,4},{6,7},{7,6},{8,9},{9,8},{10,11... | collective-permute-start | bytes 4718600 | tf_op jit(solution)/shard_map/ppermute | solution.py:34
  81.9 13.6 %collective-permute-start.2 = (bf16[384,2048]{1,0:T(8,128)(2,1)}, bf16[384,2048]{1,0:T(8,128)(2,1)}, u32[]{:S(2)}, u32[]{:S(2)}) collective-permute-start(bf16[384,2048]{1,0:T(8,128)(2,1)} %bitcast.39), channel_id=1, source_target_pairs={{0,1},{1,0},{2,3},{3,2},{4,5},{5,4},{6,7},{7,6},{8,9},{9,8},{10,11... | collective-permute-start | bytes 4718600 | tf_op jit(solution)/shard_map/ppermute | solution.py:34
  84.6 5.4 %copy-start.14 = (bf16[1,2048,384]{2,1,0:T(8,128)(2,1)S(1)}, bf16[1,2048,384]{2,1,0:T(8,128)(2,1)}, u32[]{:S(2)}) copy-start(bf16[1,2048,384]{2,1,0:T(8,128)(2,1)} %param.11) | copy-start | bytes 4718596
  89.9 5.6 %copy-start.17 = (f32[512,768]{1,0:T(8,128)}, f32[512,768]{1,0:T(8,128)S(1)}, u32[]{:S(2)}) copy-start(f32[512,768]{1,0:T(8,128)S(1)} %fusion.10) | copy-start | bytes 4718596
  89.9 6.5 %copy-start.13 = (bf16[1,384,2048]{2,1,0:T(8,128)(2,1)S(1)}, bf16[1,384,2048]{2,1,0:T(8,128)(2,1)}, u32[]{:S(2)}) copy-start(bf16[1,384,2048]{2,1,0:T(8,128)(2,1)} %param.12) | copy-start | bytes 4718596
  133.6 58.5 %all-to-all-start.2 = ((bf16[128,4,2048]{2,1,0:T(4,128)(2,1)}), bf16[128,4,2048]{2,1,0:T(4,128)(2,1)}, u32[]{:S(2)}, u32[]{:S(2)}) async-start(bf16[128,4,2048]{2,1,0:T(4,128)(2,1)} %reshape.55), calls=%async_computation.2 | async-start | bytes 4194304 | tf_op jit(solution)/shard_map/all_to_all | solution.py:15
  144.4 6.8 %copy-start.15 = (bf16[1,2048,384]{2,1,0:T(8,128)(2,1)S(1)}, bf16[1,2048,384]{2,1,0:T(8,128)(2,1)}, u32[]{:S(2)}) copy-start(bf16[1,2048,384]{2,1,0:T(8,128)(2,1)} %param.11) | copy-start | bytes 4718596
  151.1 4.2 %copy-start.7 = (bf16[512,768]{1,0:T(8,128)(2,1)}, bf16[512,768]{1,0:T(8,128)(2,1)S(1)}, u32[]{:S(2)}) copy-start(bf16[512,768]{1,0:T(8,128)(2,1)S(1)} %get-tuple-element.21) | copy-start | bytes 2359300
  151.1 4.2 %copy-start.9 = (bf16[512,768]{1,0:T(8,128)(2,1)}, bf16[512,768]{1,0:T(8,128)(2,1)S(1)}, u32[]{:S(2)}) copy-start(bf16[512,768]{1,0:T(8,128)(2,1)S(1)} %get-tuple-element.20) | copy-start | bytes 2359300
  151.1 4.2 %copy-start.16 = (bf16[1,2048,384]{2,1,0:T(8,128)(2,1)S(1)}, bf16[1,2048,384]{2,1,0:T(8,128)(2,1)}, u32[]{:S(2)}) copy-start(bf16[1,2048,384]{2,1,0:T(8,128)(2,1)} %param.10) | copy-start | bytes 4718596
  192.1 58.3 %all-to-all-start.3 = ((bf16[128,4,2048]{2,1,0:T(4,128)(2,1)}), bf16[128,4,2048]{2,1,0:T(4,128)(2,1)}, u32[]{:S(2)}, u32[]{:S(2)}) async-start(bf16[128,4,2048]{2,1,0:T(4,128)(2,1)} %reshape.57), calls=%async_computation.3 | async-start | bytes 4194304 | tf_op jit(solution)/shard_map/all_to_all | solution.py:15
  206.3 15.5 %collective-permute-start.5 = (f32[384,2048]{1,0:T(8,128)}, f32[384,2048]{1,0:T(8,128)}, u32[]{:S(2)}, u32[]{:S(2)}) collective-permute-start(f32[384,2048]{1,0:T(8,128)} %slice_select_fusion), channel_id=1, source_target_pairs={{0,1},{1,0},{2,3},{3,2},{4,5},{5,4},{6,7},{7,6},{8,9},{9,8},{10,11... | collective-permute-start | bytes 9437192 | tf_op jit(solution)/shard_map/ppermute | solution.py:93
  211.7 15.9 %collective-permute-start.3 = (f32[2048,384]{1,0:T(8,128)}, f32[2048,384]{1,0:T(8,128)}, u32[]{:S(2)}, u32[]{:S(2)}) collective-permute-start(f32[2048,384]{1,0:T(8,128)} %slice_select_fusion.2), channel_id=1, source_target_pairs={{0,1},{1,0},{2,3},{3,2},{4,5},{5,4},{6,7},{7,6},{8,9},{9,8},{10,11... | collective-permute-start | bytes 9437192 | tf_op jit(solution)/shard_map/ppermute | solution.py:93
  217.6 13.9 %collective-permute-start.4 = (f32[2048,384]{1,0:T(8,128)}, f32[2048,384]{1,0:T(8,128)}, u32[]{:S(2)}, u32[]{:S(2)}) collective-permute-start(f32[2048,384]{1,0:T(8,128)} %slice_select_fusion.1), channel_id=1, source_target_pairs={{0,1},{1,0},{2,3},{3,2},{4,5},{5,4},{6,7},{7,6},{8,9},{9,8},{10,11... | collective-permute-start | bytes 9437192 | tf_op jit(solution)/shard_map/ppermute | solution.py:93
  220.2 7.5 %slice-start.2 = ((s8[6291456]{0:T(1024)(128)(4,1)}), s8[4194304]{0:T(1024)(128)(4,1)S(1)}, s32[]{:S(2)}) async-start(s8[6291456]{0:T(1024)(128)(4,1)} %bitcast.35), calls=%async_computation.6 | async-start | bytes 8388608
  221.8 5.8 %slice-start.3 = ((s8[6291456]{0:T(1024)(128)(4,1)}), s8[2097152]{0:T(1024)(128)(4,1)S(1)}, s32[]{:S(2)}) async-start(s8[6291456]{0:T(1024)(128)(4,1)} %bitcast.35), calls=%async_computation.7 | async-start | bytes 4194304
  221.8 9.7 %slice-start = ((s8[6291456]{0:T(1024)(128)(4,1)}), s8[4194304]{0:T(1024)(128)(4,1)S(1)}, s32[]{:S(2)}) async-start(s8[6291456]{0:T(1024)(128)(4,1)} %bitcast.33), calls=%async_computation.4 | async-start | bytes 8388608
  231.5 22.6 %copy-start.1 = (bf16[128,2048]{1,0:T(8,128)(2,1)S(1)}, bf16[128,2048]{1,0:T(8,128)(2,1)}, u32[]{:S(2)}) copy-start(bf16[128,2048]{1,0:T(8,128)(2,1)} %param.7) | copy-start | bytes 1572868
  (8 other events, 25.3 us)

commit v6 on v4

--- a/solution.py
+++ b/solution.py
@@ -43,9 +43,9 @@
     wd = jnp.where(first, jnp.concatenate([w_down[0], wd_o], 0), jnp.concatenate([wd_o, w_down[0]], 0))
 
     expert_ids = routes.reshape(pairs)
-    onehot = (expert_ids[:, None] == jnp.arange(chips, dtype=jnp.int32)[None, :]).astype(jnp.int32)
-    before = jnp.cumsum(onehot, axis=0) - onehot
-    position = jnp.sum(before * onehot, axis=1)
+    order = jnp.arange(pairs, dtype=jnp.int32)
+    earlier = (expert_ids[:, None] == expert_ids[None, :]) & (order[None, :] < order[:, None])
+    position = jnp.sum(earlier.astype(jnp.int32), axis=1)
     slot = expert_ids * most + position
     gates = gate_codes.reshape(pairs).astype(f32) / 1024.0
     qpairs = (

time: 258 us -> 257 us (level)
  no operation moved by 1% of the time
where the time goes in v6:
time: 257 us; the launch traced here: 256 us
  waiting for transfers between devices  124 us (48%)
  matrix products  63.5 us (25%)
  starting transfers between devices  37 us (14%)
  local copies, waits for them, and re-layouts  29.6 us (12%)
    all_to_all x4, waiting for transfers between devices, to_chips(): return lax.all_to_all(packed, CHIPS, 0, 0, tiled=True)  124 us
    all_to_all x4, starting transfers between devices, to_chips(): return lax.all_to_all(packed, CHIPS, 0, 0, tiled=True)  35.8 us
    reshape x4, local copies, waits for them, and re-layouts, pack(): return rows.reshape(chips, -1, rows.shape[1])  14.6 us
    reshape x4, local copies, waits for them, and re-layouts, unpack(): return sent.reshape(-1, sent.shape[2])  13.1 us
    dot_general x1, matrix products, local(): dhid = jnp.dot(qrows, wd.T, preferred_element_type=f32)  6.7 us
    dot_general x1, matrix products, local(): upv = jnp.dot(xrows, wu, preferred_element_type=f32)  5.58 us
    dot_general x1, matrix products, local(): jnp.dot(dact, wg.T, preferred_element_type=f32)  5.24 us
    dot_general x1, matrix products, local(): outv = jnp.dot(hidden, wd, preferred_element_type=f32).astype(jnp.bfloat16)  5.15 us
  transfers between devices with their start and end apart: 10, of which 5 were waited for; matrix products, arithmetic and copies ran while one was open for 33% of the time, Pallas kernels for 0%

profile of v6, /device:TPU:32, one launch (start us, length us, event | category | flops | bytes accessed | tf_op | source)
XLA Modules:
  0.0 256.4 jit_solution(8557742775760496290)
XLA Ops:
  6.5 15.1 %all-to-all-start = ((bf16[128,4,2048]{2,1,0:T(4,128)(2,1)}), bf16[128,4,2048]{2,1,0:T(4,128)(2,1)S(1)}, u32[]{:S(2)}, u32[]{:S(2)}) async-start(bf16[128,4,2048]{2,1,0:T(4,128)(2,1)} %reshape.53), calls=%async_computation | async-start | bytes 4194304 | tf_op jit(solution)/shard_map/all_to_all | solution.py:15
  24.0 4.1 %reshape.52 = bf16[128,4,2048]{2,1,0:T(4,128)(2,1)} reshape(bf16[512,2048]{1,0:T(8,128)(2,1)} %bitcast_convert_fusion) | data formatting | bytes 4194304 | tf_op jit(solution)/shard_map/reshape | solution.py:11
  28.1 47.1 %all-to-all-done = bf16[128,4,2048]{2,1,0:T(4,128)(2,1)S(1)} async-done(((bf16[128,4,2048]{2,1,0:T(4,128)(2,1)}), bf16[128,4,2048]{2,1,0:T(4,128)(2,1)S(1)}, u32[]{:S(2)}, u32[]{:S(2)}) %all-to-all-start) | async-done | bytes 2097184 | tf_op jit(solution)/shard_map/all_to_all | solution.py:15
  75.1 6.9 %all-to-all-start.1 = ((bf16[128,4,2048]{2,1,0:T(4,128)(2,1)}), bf16[128,4,2048]{2,1,0:T(4,128)(2,1)}, u32[]{:S(2)}, u32[]{:S(2)}) async-start(bf16[128,4,2048]{2,1,0:T(4,128)(2,1)} %reshape.52), calls=%async_computation.1 | async-start | bytes 4194304 | tf_op jit(solution)/shard_map/all_to_all | solution.py:15
  85.8 4.9 %fusion.10 = f32[512,768]{1,0:T(8,128)S(1)} fusion(bf16[512,2048]{1,0:T(8,128)(2,1)S(1)} %reshape.54, bf16[2048,384]{1,0:T(8,128)(2,1)} %collective-permute-done, bf16[2048,384]{1,0:T(8,128)(2,1)} %bitcast.43, pred[]{:T(512)S(6)} %eq.48), kind=kOutput, calls=%fused_computation.27 | convolution fusion | flops 1624768512 | bytes 6815745 | tf_op jit(solution)/shard_map/dot_general | solution.py:69
  90.8 5.6 %multiply_convert_fusion.3 = (bf16[512,768]{1,0:T(8,128)(2,1)S(1)}, f32[512,768]{1,0:T(8,128)}) fusion(f32[512,768]{1,0:T(8,128)S(1)} %fusion.10, bf16[512,2048]{1,0:T(8,128)(2,1)S(1)} %reshape.54, bf16[2048,384]{1,0:T(8,128)(2,1)} %collective-permute-done.1, bf16[2048,384]{1,0:T(8,128)(2,1)S(1)} %bitcast.40, pred[]{:T(512)S(6)} %eq.48), kind=kOutput, calls=%fused_computation.18 | convolution fusion | flops 1627127808 | bytes 9175041 | tf_op jit(solution)/shard_map/dot_general | solution.py:70
  96.4 5.2 %convolution_convert_fusion.1 = bf16[512,2048]{1,0:T(8,128)(2,1)} fusion(bf16[512,768]{1,0:T(8,128)(2,1)S(1)} %get-tuple-element.29, bf16[384,2048]{1,0:T(8,128)(2,1)} %collective-permute-done.2, bf16[384,2048]{1,0:T(8,128)(2,1)S(1)} %bitcast.38, pred[]{:T(512)S(6)} %eq.48), kind=kOutput, calls=%fused_computation.9 | convolution fusion | flops 1625817088 | bytes 6029313 | tf_op jit(solution)/shard_map/dot_general | solution.py:74
  101.5 4.1 %reshape.55 = bf16[128,4,2048]{2,1,0:T(4,128)(2,1)} reshape(bf16[512,2048]{1,0:T(8,128)(2,1)} %convolution_convert_fusion.1) | data formatting | bytes 4194304 | tf_op jit(solution)/shard_map/reshape | solution.py:11
  105.6 28.6 %all-to-all-done.1 = bf16[128,4,2048]{2,1,0:T(4,128)(2,1)} async-done(((bf16[128,4,2048]{2,1,0:T(4,128)(2,1)}), bf16[128,4,2048]{2,1,0:T(4,128)(2,1)}, u32[]{:S(2)}, u32[]{:S(2)}) %all-to-all-start.1) | async-done | bytes 2097184 | tf_op jit(solution)/shard_map/all_to_all | solution.py:15
  134.3 6.9 %all-to-all-start.2 = ((bf16[128,4,2048]{2,1,0:T(4,128)(2,1)}), bf16[128,4,2048]{2,1,0:T(4,128)(2,1)}, u32[]{:S(2)}, u32[]{:S(2)}) async-start(bf16[128,4,2048]{2,1,0:T(4,128)(2,1)} %reshape.55), calls=%async_computation.2 | async-start | bytes 4194304 | tf_op jit(solution)/shard_map/all_to_all | solution.py:15
  141.2 4.0 %reshape.56 = bf16[512,2048]{1,0:T(8,128)(2,1)} reshape(bf16[128,4,2048]{2,1,0:T(4,128)(2,1)} %all-to-all-done.1) | data formatting | bytes 4194304 | tf_op jit(solution)/shard_map/reshape | solution.py:19
  145.2 6.7 %multiply_convert_fusion.2 = (bf16[512,768]{1,0:T(8,128)(2,1)S(1)}, bf16[512,768]{1,0:T(8,128)(2,1)S(1)}) fusion(f32[512,768]{1,0:T(8,128)} %copy-done.16, f32[512,768]{1,0:T(8,128)} %get-tuple-element.30, bf16[512,2048]{1,0:T(8,128)(2,1)} %reshape.56, bf16[384,2048]{1,0:T(8,128)(2,1)} %collective-permute-done.2, bf16[384,2048]{1,0:T(8,128)(2,1)} %bitcast.37, ...), kind=kOutput, calls=%fused_computation.17 | convolution fusion | flops 1629880320 | bytes 9961473 | tf_op jit(solution)/shard_map/dot_general | solution.py:79
  151.9 4.2 %fusion.8 = f32[512,2048]{1,0:T(8,128)S(1)} fusion(bf16[512,768]{1,0:T(8,128)(2,1)S(1)} %get-tuple-element.22, bf16[2048,384]{1,0:T(8,128)(2,1)} %collective-permute-done.1, bf16[2048,384]{1,0:T(8,128)(2,1)S(1)} %bitcast.41, pred[]{:T(512)S(6)} %eq.48), kind=kOutput, calls=%fused_computation.25 | convolution fusion | flops 1624768512 | bytes 8126465 | tf_op jit(solution)/shard_map/dot_general | solution.py:84
  156.1 5.2 %add_convert_fusion = bf16[512,2048]{1,0:T(8,128)(2,1)} fusion(f32[512,2048]{1,0:T(8,128)S(1)} %fusion.8, bf16[512,768]{1,0:T(8,128)(2,1)S(1)} %get-tuple-element.21, bf16[2048,384]{1,0:T(8,128)(2,1)} %collective-permute-done, bf16[2048,384]{1,0:T(8,128)(2,1)S(1)} %bitcast.44, pred[]{:T(512)S(6)} %eq.48), kind=kOutput, calls=%fused_computation.1 | convolution fusion | flops 1626865664 | bytes 10223617 | tf_op jit(solution)/shard_map/dot_general | solution.py:83
  161.3 4.1 %reshape.57 = bf16[128,4,2048]{2,1,0:T(4,128)(2,1)} reshape(bf16[512,2048]{1,0:T(8,128)(2,1)} %add_convert_fusion) | data formatting | bytes 4194304 | tf_op jit(solution)/shard_map/reshape | solution.py:11
  165.5 4.2 %fusion.18 = f32[384,2048]{1,0:T(8,128)} fusion(bf16[512,2048]{1,0:T(8,128)(2,1)} %reshape.56, pred[]{:T(512)S(6)} %eq.48, bf16[512,768]{1,0:T(8,128)(2,1)S(1)} %get-tuple-element.29), kind=kOutput, calls=%fused_computation.37 | convolution fusion | flops 805502976 | bytes 6029313 | tf_op jit(solution)/shard_map/dot_general | solution.py:87
  169.7 23.1 %all-to-all-done.2 = bf16[128,4,2048]{2,1,0:T(4,128)(2,1)} async-done(((bf16[128,4,2048]{2,1,0:T(4,128)(2,1)}), bf16[128,4,2048]{2,1,0:T(4,128)(2,1)}, u32[]{:S(2)}, u32[]{:S(2)}) %all-to-all-start.2) | async-done | bytes 2097184 | tf_op jit(solution)/shard_map/all_to_all | solution.py:15
  192.8 6.9 %all-to-all-start.3 = ((bf16[128,4,2048]{2,1,0:T(4,128)(2,1)}), bf16[128,4,2048]{2,1,0:T(4,128)(2,1)}, u32[]{:S(2)}, u32[]{:S(2)}) async-start(bf16[128,4,2048]{2,1,0:T(4,128)(2,1)} %reshape.57), calls=%async_computation.3 | async-start | bytes 4194304 | tf_op jit(solution)/shard_map/all_to_all | solution.py:15
  199.8 4.2 %fusion.15 = f32[2048,384]{1,0:T(8,128)} fusion(bf16[512,2048]{1,0:T(8,128)(2,1)S(1)} %reshape.54, pred[]{:T(512)S(6)} %eq.48, bf16[512,768]{1,0:T(8,128)(2,1)} %copy-done.8), kind=kOutput, calls=%fused_computation.34 | convolution fusion | flops 805502976 | bytes 6029313 | tf_op jit(solution)/shard_map/dot_general | solution.py:97
  207.4 4.0 %reshape.61 = bf16[512,2048,1]{1,0,2:T(8,128)(2,1)} reshape(bf16[128,4,2048]{2,1,0:T(4,128)(2,1)} %all-to-all-done.2) | data formatting | bytes 4194304 | tf_op jit(solution)/shard_map/reshape | solution.py:19
  214.9 4.1 %fusion.2 = bf16[1,384,2048]{2,1,0:T(8,128)(2,1)} fusion(f32[384,2048]{1,0:T(8,128)} %collective-permute-done.5, bf16[512,384]{1,0:T(8,128)(2,1)S(1)} %broadcast_select_fusion, bf16[512,2048]{1,0:T(8,128)(2,1)S(1)} %copy-done.2), kind=kOutput, calls=%fused_computation.13 | convolution fusion | flops 806879232 | bytes 7208960 | tf_op jit(solution)/shard_map/dot_general | solution.py:104
  219.0 4.3 %fusion = bf16[1,2048,384]{2,1,0:T(8,128)(2,1)} fusion(f32[2048,384]{1,0:T(8,128)} %collective-permute-done.3, bf16[512,2048]{1,0:T(8,128)(2,1)S(1)} %reshape.54, pred[]{:T(512)S(6)} %eq.48, bf16[512,768]{1,0:T(8,128)(2,1)S(1)} %copy-done.9), kind=kOutput, calls=%fused_computation.11 | convolution fusion | flops 807075840 | bytes 7602177 | tf_op jit(solution)/shard_map/dot_general | solution.py:102
  223.3 4.3 %fusion.1 = bf16[1,2048,384]{2,1,0:T(8,128)(2,1)} fusion(f32[2048,384]{1,0:T(8,128)} %collective-permute-done.4, bf16[512,2048]{1,0:T(8,128)(2,1)S(1)} %reshape.54, pred[]{:T(512)S(6)} %eq.48, bf16[512,768]{1,0:T(8,128)(2,1)S(1)} %copy-done.7), kind=kOutput, calls=%fused_computation.12 | convolution fusion | flops 807075840 | bytes 7602177 | tf_op jit(solution)/shard_map/dot_general | solution.py:103
  227.7 24.8 %all-to-all-done.3 = bf16[128,4,2048]{2,1,0:T(4,128)(2,1)} async-done(((bf16[128,4,2048]{2,1,0:T(4,128)(2,1)}), bf16[128,4,2048]{2,1,0:T(4,128)(2,1)}, u32[]{:S(2)}, u32[]{:S(2)}) %all-to-all-start.3) | async-done | bytes 2097184 | tf_op jit(solution)/shard_map/all_to_all | solution.py:15
  (64 shorter events, 22.8 us)
Async XLA Ops:
  6.5 15.2 %copy-start.10 = (bf16[128,2048]{1,0:T(8,128)(2,1)S(1)}, bf16[128,2048]{1,0:T(8,128)(2,1)}, u32[]{:S(2)}) copy-start(bf16[128,2048]{1,0:T(8,128)(2,1)} %param.13) | copy-start | bytes 1572868
  6.5 15.3 %copy-start.11 = (s32[128,2]{0,1:T(2,128)S(1)}, s32[128,2]{0,1:T(2,128)}, u32[]{:S(2)}) copy-start(s32[128,2]{0,1:T(2,128)} %param.9) | copy-start | bytes 3076
  6.5 68.6 %all-to-all-start = ((bf16[128,4,2048]{2,1,0:T(4,128)(2,1)}), bf16[128,4,2048]{2,1,0:T(4,128)(2,1)S(1)}, u32[]{:S(2)}, u32[]{:S(2)}) async-start(bf16[128,4,2048]{2,1,0:T(4,128)(2,1)} %reshape.53), calls=%async_computation | async-start | bytes 4194304 | tf_op jit(solution)/shard_map/all_to_all | solution.py:15
  75.1 6.9 %copy-start.3 = (bf16[128,4,2048]{2,1,0:T(4,128)(2,1)}, bf16[128,4,2048]{2,1,0:T(4,128)(2,1)S(1)}, u32[]{:S(2)}) copy-start(bf16[128,4,2048]{2,1,0:T(4,128)(2,1)S(1)} %all-to-all-done) | copy-start | bytes 6291460
  75.1 59.1 %all-to-all-start.1 = ((bf16[128,4,2048]{2,1,0:T(4,128)(2,1)}), bf16[128,4,2048]{2,1,0:T(4,128)(2,1)}, u32[]{:S(2)}, u32[]{:S(2)}) async-start(bf16[128,4,2048]{2,1,0:T(4,128)(2,1)} %reshape.52), calls=%async_computation.1 | async-start | bytes 4194304 | tf_op jit(solution)/shard_map/all_to_all | solution.py:15
  82.0 3.8 %collective-permute-start = (bf16[2048,384]{1,0:T(8,128)(2,1)}, bf16[2048,384]{1,0:T(8,128)(2,1)}, u32[]{:S(2)}, u32[]{:S(2)}) collective-permute-start(bf16[2048,384]{1,0:T(8,128)(2,1)} %bitcast.42), channel_id=1, source_target_pairs={{0,1},{1,0},{2,3},{3,2},{4,5},{5,4},{6,7},{7,6},{8,9},{9,8},{10,11... | collective-permute-start | bytes 4718600 | tf_op jit(solution)/shard_map/ppermute | solution.py:34
  82.1 8.7 %collective-permute-start.1 = (bf16[2048,384]{1,0:T(8,128)(2,1)}, bf16[2048,384]{1,0:T(8,128)(2,1)}, u32[]{:S(2)}, u32[]{:S(2)}) collective-permute-start(bf16[2048,384]{1,0:T(8,128)(2,1)} %bitcast.39), channel_id=1, source_target_pairs={{0,1},{1,0},{2,3},{3,2},{4,5},{5,4},{6,7},{7,6},{8,9},{9,8},{10,11... | collective-permute-start | bytes 4718600 | tf_op jit(solution)/shard_map/ppermute | solution.py:34
  82.6 13.8 %collective-permute-start.2 = (bf16[384,2048]{1,0:T(8,128)(2,1)}, bf16[384,2048]{1,0:T(8,128)(2,1)}, u32[]{:S(2)}, u32[]{:S(2)}) collective-permute-start(bf16[384,2048]{1,0:T(8,128)(2,1)} %bitcast.36), channel_id=1, source_target_pairs={{0,1},{1,0},{2,3},{3,2},{4,5},{5,4},{6,7},{7,6},{8,9},{9,8},{10,11... | collective-permute-start | bytes 4718600 | tf_op jit(solution)/shard_map/ppermute | solution.py:34
  85.2 5.5 %copy-start.13 = (bf16[1,2048,384]{2,1,0:T(8,128)(2,1)S(1)}, bf16[1,2048,384]{2,1,0:T(8,128)(2,1)}, u32[]{:S(2)}) copy-start(bf16[1,2048,384]{2,1,0:T(8,128)(2,1)} %param.11) | copy-start | bytes 4718596
  90.7 5.6 %copy-start.16 = (f32[512,768]{1,0:T(8,128)}, f32[512,768]{1,0:T(8,128)S(1)}, u32[]{:S(2)}) copy-start(f32[512,768]{1,0:T(8,128)S(1)} %fusion.10) | copy-start | bytes 4718596
  90.7 5.6 %copy-start.12 = (bf16[1,384,2048]{2,1,0:T(8,128)(2,1)S(1)}, bf16[1,384,2048]{2,1,0:T(8,128)(2,1)}, u32[]{:S(2)}) copy-start(bf16[1,384,2048]{2,1,0:T(8,128)(2,1)} %param.12) | copy-start | bytes 4718596
  134.3 58.6 %all-to-all-start.2 = ((bf16[128,4,2048]{2,1,0:T(4,128)(2,1)}), bf16[128,4,2048]{2,1,0:T(4,128)(2,1)}, u32[]{:S(2)}, u32[]{:S(2)}) async-start(bf16[128,4,2048]{2,1,0:T(4,128)(2,1)} %reshape.55), calls=%async_computation.2 | async-start | bytes 4194304 | tf_op jit(solution)/shard_map/all_to_all | solution.py:15
  145.2 6.7 %copy-start.14 = (bf16[1,2048,384]{2,1,0:T(8,128)(2,1)S(1)}, bf16[1,2048,384]{2,1,0:T(8,128)(2,1)}, u32[]{:S(2)}) copy-start(bf16[1,2048,384]{2,1,0:T(8,128)(2,1)} %param.11) | copy-start | bytes 4718596
  151.9 4.2 %copy-start.6 = (bf16[512,768]{1,0:T(8,128)(2,1)}, bf16[512,768]{1,0:T(8,128)(2,1)S(1)}, u32[]{:S(2)}) copy-start(bf16[512,768]{1,0:T(8,128)(2,1)S(1)} %get-tuple-element.22) | copy-start | bytes 2359300
  151.9 4.2 %copy-start.8 = (bf16[512,768]{1,0:T(8,128)(2,1)}, bf16[512,768]{1,0:T(8,128)(2,1)S(1)}, u32[]{:S(2)}) copy-start(bf16[512,768]{1,0:T(8,128)(2,1)S(1)} %get-tuple-element.21) | copy-start | bytes 2359300
  151.9 4.2 %copy-start.15 = (bf16[1,2048,384]{2,1,0:T(8,128)(2,1)S(1)}, bf16[1,2048,384]{2,1,0:T(8,128)(2,1)}, u32[]{:S(2)}) copy-start(bf16[1,2048,384]{2,1,0:T(8,128)(2,1)} %param.10) | copy-start | bytes 4718596
  192.8 22.0 %collective-permute-start.5 = (f32[384,2048]{1,0:T(8,128)}, f32[384,2048]{1,0:T(8,128)}, u32[]{:S(2)}, u32[]{:S(2)}) collective-permute-start(f32[384,2048]{1,0:T(8,128)} %fusion.18), channel_id=1, source_target_pairs={{0,1},{1,0},{2,3},{3,2},{4,5},{5,4},{6,7},{7,6},{8,9},{9,8},{10,11... | collective-permute-start | bytes 9437192 | tf_op jit(solution)/shard_map/ppermute | solution.py:101
  192.8 59.7 %all-to-all-start.3 = ((bf16[128,4,2048]{2,1,0:T(4,128)(2,1)}), bf16[128,4,2048]{2,1,0:T(4,128)(2,1)}, u32[]{:S(2)}, u32[]{:S(2)}) async-start(bf16[128,4,2048]{2,1,0:T(4,128)(2,1)} %reshape.57), calls=%async_computation.3 | async-start | bytes 4194304 | tf_op jit(solution)/shard_map/all_to_all | solution.py:15
  199.8 4.3 %copy-start.7 = (bf16[512,768]{1,0:T(8,128)(2,1)S(1)}, bf16[512,768]{1,0:T(8,128)(2,1)}, u32[]{:S(2)}) copy-start(bf16[512,768]{1,0:T(8,128)(2,1)} %copy-done.6) | copy-start | bytes 2359300
  204.0 15.0 %collective-permute-start.3 = (f32[2048,384]{1,0:T(8,128)}, f32[2048,384]{1,0:T(8,128)}, u32[]{:S(2)}, u32[]{:S(2)}) collective-permute-start(f32[2048,384]{1,0:T(8,128)} %fusion.15), channel_id=1, source_target_pairs={{0,1},{1,0},{2,3},{3,2},{4,5},{5,4},{6,7},{7,6},{8,9},{9,8},{10,11... | collective-permute-start | bytes 9437192 | tf_op jit(solution)/shard_map/ppermute | solution.py:101
  206.9 16.4 %collective-permute-start.4 = (f32[2048,384]{1,0:T(8,128)}, f32[2048,384]{1,0:T(8,128)}, u32[]{:S(2)}, u32[]{:S(2)}) collective-permute-start(f32[2048,384]{1,0:T(8,128)} %fusion.12), channel_id=1, source_target_pairs={{0,1},{1,0},{2,3},{3,2},{4,5},{5,4},{6,7},{7,6},{8,9},{9,8},{10,11... | collective-permute-start | bytes 9437192 | tf_op jit(solution)/shard_map/ppermute | solution.py:101
  214.9 4.2 %copy-start.9 = (bf16[512,768]{1,0:T(8,128)(2,1)S(1)}, bf16[512,768]{1,0:T(8,128)(2,1)}, u32[]{:S(2)}) copy-start(bf16[512,768]{1,0:T(8,128)(2,1)} %copy-done.8) | copy-start | bytes 2359300
  227.7 27.4 %copy-start.5 = (bf16[2,128,512]{2,1,0:T(8,128)(2,1)S(1)}, bf16[2,128,512]{2,1,0:T(8,128)(2,1)}, u32[]{:S(2)}) copy-start(bf16[2,128,512]{2,1,0:T(8,128)(2,1)} %copy-done.4) | copy-start | bytes 786436
  252.5 3.9 %copy-start.1 = (bf16[128,2048]{1,0:T(8,128)(2,1)S(1)}, bf16[128,2048]{1,0:T(8,128)(2,1)}, u32[]{:S(2)}) copy-start(bf16[128,2048]{1,0:T(8,128)(2,1)} %param.7) | copy-start | bytes 1572868
  (3 other events, 7.1 us)
